TPU v7x, 128 devices: a whole 4x4x4 slice. The times are simulated.
128 devices in a mesh: gop: 8 (over z, core), row: 16 (over x, y).
Axes of the slice: x: 4, y: 4, z: 4, core: 2. Of those that a mesh axis runs over, the one named last changes fastest.
Arguments:
- features: bfloat16 [8, 256, 480, 128], P('gop', 'row'), may hold values from -6 to 6
- filters: bfloat16 [3, 256, 2, 480, 128], P(None, None, None, 'row'), may hold values from -2.390625 to 2.390625
- anchors: int32 [8, 2], replicated, may hold values from 0 to 7, as said below
Outputs:
- joined: bfloat16 [8, 256, 480, 128], P('gop', 'row')
Inputs may be any that keep to these rules, and one draw needn't show every extreme that they name: anchors[:, 0] lists each of the 8 frames exactly once; anchors[:, 1] takes exactly two distinct values, each in half of the rows.
All inputs are finite; a program needn't handle non-finite values.
Results may differ from a plain program's by a relative error of at most 0.0062.
Values may be sent and summed in bfloat16 or wider, within the bound.
No kernel may reach another device: no remote copies, remote signals or barrier semaphores. Data moves between devices by JAX's collectives and lax.ppermute only.
A program may use at most 256 MiB of HBM per device.

v0:
```python
import math

import jax
import jax.numpy as jnp
from jax import lax
from jax.sharding import PartitionSpec as P


def row_table(length):
    across = jnp.arange(length, dtype=jnp.int32)
    phases = across[:, None] * across[None, :] % length
    angles = phases.astype(jnp.float32) * (2.0 * math.pi / length)
    factor = 1.0 / math.sqrt(length)
    return jnp.concatenate([jnp.cos(angles) * factor, -jnp.sin(angles) * factor], axis=1).astype(
        jnp.bfloat16
    )


def column_matrix(length, sign):
    across = jnp.arange(length, dtype=jnp.int32)
    phases = across[:, None] * across[None, :] % length
    angles = phases.astype(jnp.float32) * (2.0 * math.pi / length)
    factor = 1.0 / math.sqrt(length)
    cosine = jnp.cos(angles) * factor
    sine_part = sign * jnp.sin(angles) * factor
    upper = jnp.stack([cosine, -sine_part], axis=-1)
    lower = jnp.stack([sine_part, cosine], axis=-1)
    return jnp.stack([upper, lower], axis=1).reshape(2 * length, 2 * length).astype(jnp.bfloat16)


def on_device(features, filters, anchors):
    frames_here = features.shape[0]
    columns = features.shape[2]
    height = filters.shape[1]
    forward_rows = row_table(columns)
    split_table = forward_rows.reshape(columns, 2, columns)
    forward_cols = column_matrix(height, -1.0)
    inverse_cols = column_matrix(height, 1.0)
    first_frame = lax.axis_index("gop") * frames_here
    own_anchors = lax.dynamic_slice_in_dim(anchors, first_frame, frames_here, 0)
    empty = jnp.zeros_like(features)
    totals = (empty, empty)
    shards = lax.all_gather(features, "gop", axis=0, tiled=True)
    amount = shards.shape[0]
    results = []
    for anchor_slot in range(2):
        wanted = own_anchors[:, anchor_slot]
        inside = jnp.logical_and(wanted >= 0, wanted < amount)
        position = jnp.clip(wanted, 0, amount - 1)
        picked = jnp.take(shards, position, axis=0)
        inside = inside.reshape((-1,) + (1,) * (shards.ndim - 1))
        results.append(jnp.where(inside, picked, totals[anchor_slot]))
    first_anchor = results[0]
    second_anchor = results[1]
    frames_in = jnp.concatenate([features, first_anchor, second_anchor], axis=0)
    count = frames_in.shape[0]
    done = jnp.einsum("nhwc,wk->nhkc", frames_in, forward_rows, preferred_element_type=jnp.float32)
    slab = lax.all_to_all(
        done.astype(jnp.bfloat16).reshape(
            count, frames_in.shape[1], 2, columns, frames_in.shape[3]
        ),
        "row",
        split_axis=3,
        concat_axis=1,
        tiled=True,
    )
    shape_in = slab.shape
    merged = slab.reshape(shape_in[0], 2 * shape_in[1], shape_in[3] * shape_in[4])

    def one_frame(matrix):
        return jnp.dot(forward_cols, matrix, preferred_element_type=jnp.float32).astype(
            jnp.bfloat16
        )

    spectra = lax.map(one_frame, merged).reshape(shape_in)
    own_spec = spectra[:frames_here]
    first_spec = spectra[frames_here : 2 * frames_here]
    second_spec = spectra[2 * frames_here :]
    sources = (own_spec, first_spec, second_spec)
    real_part = jnp.zeros(own_spec[:, :, 0].shape, jnp.float32)
    imag_part = jnp.zeros(own_spec[:, :, 0].shape, jnp.float32)
    for which_one in range(3):
        source_real = sources[which_one][:, :, 0].astype(jnp.float32)
        source_imag = sources[which_one][:, :, 1].astype(jnp.float32)
        gain_real = filters[which_one, :, 0].astype(jnp.float32)
        gain_imag = filters[which_one, :, 1].astype(jnp.float32)
        real_part = real_part + gain_real * source_real - gain_imag * source_imag
        imag_part = imag_part + gain_real * source_imag + gain_imag * source_real
    mixed = jnp.stack([real_part, imag_part], axis=2).astype(jnp.bfloat16)
    mixed_shape = mixed.shape
    merged = mixed.reshape(mixed_shape[0], 2 * mixed_shape[1], mixed_shape[3] * mixed_shape[4])

    def invert_frame(matrix):
        return jnp.dot(inverse_cols, matrix, preferred_element_type=jnp.float32).astype(
            jnp.bfloat16
        )

    back = lax.map(invert_frame, merged).reshape(mixed_shape)
    spatial = jnp.einsum(
        "nhpkc,wpk->nhwc",
        lax.all_to_all(back, "row", split_axis=1, concat_axis=3, tiled=True),
        split_table,
        preferred_element_type=jnp.float32,
    )
    return (features.astype(jnp.float32) + spatial).astype(jnp.bfloat16)


def solution(mesh):
    in_specs = (P("gop", "row", None, None), P(None, None, None, "row", None), P())
    out_specs = P("gop", "row", None, None)
    return jax.shard_map(
        on_device, mesh=mesh, in_specs=in_specs, out_specs=out_specs, check_vma=False
    )
```

profile of v0, /device:TPU:0, one launch (start us, length us, event | category | flops | bytes accessed | tf_op | source)
XLA Modules:
  0.0 551.1 jit_solution(13978895081036516332)
XLA Ops:
  6.5 0.0 copy-start
  6.5 0.0 all-gather.2.cloned.1.call-start
  6.5 0.7 all-gather.2.cloned.1.call-update
  7.3 0.0 copy-done
  7.3 0.1 constant_dynamic-slice_fusion
  7.3 0.6 fusion.58
  11.9 4.3 multiply_convert_fusion
  16.2 76.1 %all-gather.2.cloned.1.call-done = bf16[8,16,480,128]{3,2,1,0:T(8,128)(2,1)} async-done(((bf16[1,16,480,128]{3,2,1,0:T(8,128)(2,1)}), bf16[8,16,480,128]{3,2,1,0:T(8,128)(2,1)}) %all-gather.2.cloned.1.call-update) | async-done | bytes 15728656 | tf_op jit(solution)/shard_map/all_gather | solution.py:43
  92.3 0.0 copy-start.2
  92.3 2.7 select_select_fusion.1
  95.0 0.0 copy-done.2
  95.0 6.5 %convolution_convert_fusion.1 = bf16[960,3,16,128]{3,0,2,1:T(8,128)(2,1)S(1)} fusion(bf16[1,16,480,128]{3,2,1,0:T(8,128)(2,1)S(1)} %get-tuple-element.63, bf16[1,16,480,128]{3,2,1,0:T(8,128)(2,1)S(1)} %get-tuple-element.62, bf16[1,16,480,128]{3,2,1,0:T(8,128)(2,1)S(1)} %copy-done.2, bf16[480,480]{0,1:T(8,128)(2,1)S(1)} %get-tuple-element.79, ...), kind=kOutput, calls=%fused_computation.6 | convolution fusion | flops 5687746560 | bytes 18616320 | tf_op jit(solution)/shard_map/nhwc,wk->nhkc/dot_general | solution.py:57
  101.5 27.6 %copy.46 = bf16[3,16,2,480,128]{4,1,2,0,3:T(8,128)(2,1)} copy(bf16[3,16,2,480,128]{4,3,2,1,0:T(8,128)(2,1)S(1)} %bitcast.69) | data formatting | bytes 23592960 | tf_op jit(solution)/shard_map/reshape | solution.py:59
  129.1 7.3 %all-to-all-start = ((bf16[3,16,2,480,128]{4,1,2,0,3:T(8,128)(2,1)}), bf16[3,16,2,480,128]{4,1,2,0,3:T(8,128)(2,1)}, u32[]{:S(2)}, u32[]{:S(2)}) async-start(bf16[3,16,2,480,128]{4,1,2,0,3:T(8,128)(2,1)} %copy.46), calls=%async_computation | async-start | bytes 23592960 | tf_op jit(solution)/shard_map/all_to_all | solution.py:58
  136.4 1.0 multiply_convert_fusion.4
  137.4 1.0 multiply_convert_fusion.5
  138.4 1.0 multiply_convert_fusion.6
  139.4 1.0 negate_convert_fusion
  140.4 1.0 negate_convert_fusion.1
  141.4 0.1 fusion.46
  141.5 0.1 pad_maximum_fusion.1
  141.6 22.2 %copy.49 = bf16[256,2,256,2]{3,2,1,0:T(8,128)(2,1)} copy(bf16[256,2,256,2]{2,0,3,1:T(8,128)(2,1)S(1)} %get-tuple-element.82) | data formatting | bytes 1048576 | tf_op jit(solution)/shard_map/stack | solution.py:28
  163.8 48.9 %convert_element_type.213 = bf16[512,512]{1,0:T(8,128)(2,1)S(1)} reshape(bf16[256,2,256,2]{3,2,1,0:T(8,128)(2,1)} %copy.49) | data formatting | bytes 1048576 | tf_op jit(solution)/shard_map/convert_element_type | solution.py:28
  212.7 22.2 %copy.44 = bf16[256,2,256,2]{3,2,1,0:T(8,128)(2,1)} copy(bf16[256,2,256,2]{2,0,3,1:T(8,128)(2,1)S(1)} %get-tuple-element.81) | data formatting | bytes 1048576 | tf_op jit(solution)/shard_map/stack | solution.py:28
  234.9 48.9 %convert_element_type.208 = bf16[512,512]{1,0:T(8,128)(2,1)S(1)} reshape(bf16[256,2,256,2]{3,2,1,0:T(8,128)(2,1)} %copy.44) | data formatting | bytes 1048576 | tf_op jit(solution)/shard_map/convert_element_type | solution.py:28
  283.8 26.3 %fusion.56 = (bf16[1,256,1,30,128]{4,2,3,1,0:T(2,128)(2,1)}, bf16[1,256,1,30,128]{4,2,3,1,0:T(2,128)(2,1)}, bf16[1,256,1,30,128]{4,2,3,1,0:T(2,128)(2,1)}, bf16[...) fusion(bf16[3,256,2,30,128]{4,2,3,1,0:T(2,128)(2,1)} %param.8), kind=kLoop, calls=%fused_computation.98 | loop fusion | bytes 23592960 | tf_op jit(solution)/shard_map/slice | solution.py:85
  310.1 30.2 %all-to-all-done = bf16[3,16,2,480,128]{4,1,2,0,3:T(8,128)(2,1)} async-done(((bf16[3,16,2,480,128]{4,1,2,0,3:T(8,128)(2,1)}), bf16[3,16,2,480,128]{4,1,2,0,3:T(8,128)(2,1)}, u32[]{:S(2)}, u32[]{:S(2)}) %all-to-all-start) | async-done | bytes 11796512 | tf_op jit(solution)/shard_map/all_to_all | solution.py:58
  340.2 13.5 %copy.48 = bf16[3,16,16,2,30,128]{5,4,3,2,1,0:T(8,128)(2,1)} copy(bf16[3,16,16,2,30,128]{5,2,3,0,4,1:T(8,128)(2,1)} %bitcast.20) | data formatting | bytes 23592960 | tf_op jit(solution)/shard_map/all_to_all | solution.py:58
  353.7 18.9 %reshape.309 = bf16[3,512,3840]{2,1,0:T(8,128)(2,1)} reshape(bf16[3,16,16,2,30,128]{5,4,3,2,1,0:T(8,128)(2,1)} %copy.48) | data formatting | bytes 23592960 | tf_op jit(solution)/shard_map/reshape | solution.py:68
  372.6 18.8 %while.3 = (s32[]{:T(128)}, bf16[3,512,3840]{1,2,0:T(8,128)(2,1)}, bf16[3,512,3840]{2,1,0:T(8,128)(2,1)}, bf16[512,512]{1,0:T(8,128)(2,1)S(1)}, s32[]{:T(128)}) while((s32[]{:T(128)}, bf16[3,512,3840]{1,2,0:T(8,128)(2,1)}, bf16[3,512,3840]{2,1,0:T(8,128)(2,1)}, bf16[512,512]{1,0:T(8,128)(2,1)S(1)}, s32[]{:T(128)}) %tuple.42), condition=%wide.region_1.3_spmd, body=%wide.region_0.2_spmd.sunk | while | flops 2015232000 | bytes 8389693 | solution.py:75
  372.6 6.3 %fusion.66 = bf16[3,512,3840]{1,2,0:T(8,128)(2,1)} fusion(bf16[3,512,3840]{1,2,0:T(8,128)(2,1)} %get-tuple-element.116, s32[]{:T(128)} %get-tuple-element.115, bf16[512,512]{1,0:T(8,128)(2,1)S(1)} %get-tuple-element.123, bf16[3,512,3840]{2,1,0:T(8,128)(2,1)} %get-tuple-element.122), kind=kOutput, calls=%fused_computation.2.clone.1 | convolution fusion | flops 2015232000 | bytes 8389632 | tf_op jit(solution)/shard_map/while/body/eval_jaxpr/dot_general | solution.py:71
  378.9 6.2 %fusion.66 = bf16[3,512,3840]{1,2,0:T(8,128)(2,1)} fusion(bf16[3,512,3840]{1,2,0:T(8,128)(2,1)} %get-tuple-element.116, s32[]{:T(128)} %get-tuple-element.115, bf16[512,512]{1,0:T(8,128)(2,1)S(1)} %get-tuple-element.123, bf16[3,512,3840]{2,1,0:T(8,128)(2,1)} %get-tuple-element.122), kind=kOutput, calls=%fused_computation.2.clone.1 | convolution fusion | flops 2015232000 | bytes 8389632 | tf_op jit(solution)/shard_map/while/body/eval_jaxpr/dot_general | solution.py:71
  385.1 6.2 %fusion.66 = bf16[3,512,3840]{1,2,0:T(8,128)(2,1)} fusion(bf16[3,512,3840]{1,2,0:T(8,128)(2,1)} %get-tuple-element.116, s32[]{:T(128)} %get-tuple-element.115, bf16[512,512]{1,0:T(8,128)(2,1)S(1)} %get-tuple-element.123, bf16[3,512,3840]{2,1,0:T(8,128)(2,1)} %get-tuple-element.122), kind=kOutput, calls=%fused_computation.2.clone.1 | convolution fusion | flops 2015232000 | bytes 8389632 | tf_op jit(solution)/shard_map/while/body/eval_jaxpr/dot_general | solution.py:71
  391.4 8.4 %fusion.57 = (bf16[1,512,3840]{1,2,0:T(8,128)(2,1)}, bf16[1,512,3840]{1,2,0:T(8,128)(2,1)}, bf16[1,512,3840]{1,2,0:T(8,128)(2,1)}) fusion(bf16[3,512,3840]{1,2,0:T(8,128)(2,1)} %get-tuple-element.40), kind=kLoop, calls=%fused_computation.99 | loop fusion | bytes 23592960 | tf_op jit(solution)/shard_map/slice | solution.py:76
  399.8 6.3 %copy.50 = bf16[1,512,3840]{2,1,0:T(8,128)(2,1)} copy(bf16[1,512,3840]{1,2,0:T(8,128)(2,1)} %get-tuple-element.70) | data formatting | bytes 7864320 | tf_op jit(solution)/shard_map/slice | solution.py:76
  406.1 7.2 %slice.64 = bf16[1,256,2,30,128]{4,3,2,1,0:T(8,128)(2,1)} reshape(bf16[1,512,3840]{2,1,0:T(8,128)(2,1)} %copy.50) | data formatting | bytes 7864320 | tf_op jit(solution)/shard_map/slice | solution.py:76
  413.3 6.3 %copy.53 = bf16[1,512,3840]{2,1,0:T(8,128)(2,1)} copy(bf16[1,512,3840]{1,2,0:T(8,128)(2,1)} %get-tuple-element.72) | data formatting | bytes 7864320 | tf_op jit(solution)/shard_map/slice | solution.py:77
  419.5 7.3 %slice.70 = bf16[1,256,2,30,128]{4,3,2,1,0:T(8,128)(2,1)} reshape(bf16[1,512,3840]{2,1,0:T(8,128)(2,1)} %copy.53) | data formatting | bytes 7864320 | tf_op jit(solution)/shard_map/slice | solution.py:77
  426.8 6.2 %copy.56 = bf16[1,512,3840]{2,1,0:T(8,128)(2,1)} copy(bf16[1,512,3840]{1,2,0:T(8,128)(2,1)} %get-tuple-element.71) | data formatting | bytes 7864320 | tf_op jit(solution)/shard_map/slice | solution.py:78
  433.0 7.2 %slice.76 = bf16[1,256,2,30,128]{4,3,2,1,0:T(8,128)(2,1)} reshape(bf16[1,512,3840]{2,1,0:T(8,128)(2,1)} %copy.56) | data formatting | bytes 7864320 | tf_op jit(solution)/shard_map/slice | solution.py:78
  440.2 14.0 %fusion.15 = (bf16[1,256,1,30,128]{4,3,2,1,0:T(8,128)(2,1)S(1)}, bf16[1,256,1,30,128]{4,3,2,1,0:T(8,128)(2,1)S(1)}) fusion(bf16[1,256,2,30,128]{4,3,2,1,0:T(8,128)(2,1)} %slice.76, bf16[1,256,2,30,128]{4,3,2,1,0:T(8,128)(2,1)} %slice.70, bf16[1,256,2,30,128]{4,3,2,1,0:T(8,128)(2,1)} %slice.64, bf16[1,256,1,30,128]{4,2,3,1,0:T(2,128)(2,1)} %get-tuple-element.69, ...), kind=kLoop, calls=%fused_computation.30 | loop fusion | flops 35389440 | bytes 27525120 | tf_op jit(solution)/shard_map/convert
  454.2 0.4 pad_maximum_fusion
  454.7 4.3 convolution_convert_fusion.2
  459.0 7.4 %reshape.310 = bf16[1,256,2,30,128]{4,3,2,1,0:T(8,128)(2,1)} reshape(bf16[512,3840]{1,0:T(8,128)(2,1)} %convolution_convert_fusion.2) | data formatting | bytes 7864320 | tf_op jit(solution)/shard_map/reshape | solution.py:98
  466.4 8.1 %copy.58 = bf16[1,256,2,30,128]{4,2,3,0,1:T(2,128)(2,1)} copy(bf16[1,256,2,30,128]{4,3,2,1,0:T(8,128)(2,1)} %reshape.310) | data formatting | bytes 7864320 | tf_op jit(solution)/shard_map/reshape | solution.py:98
  474.5 10.4 %all-to-all-start.1 = ((bf16[1,256,2,30,128]{4,2,3,0,1:T(2,128)(2,1)}), bf16[1,256,2,30,128]{4,2,3,0,1:T(2,128)(2,1)}, u32[]{:S(2)}, u32[]{:S(2)}) async-start(bf16[1,256,2,30,128]{4,2,3,0,1:T(2,128)(2,1)} %copy.58), calls=%async_computation.1 | async-start | bytes 7864320 | tf_op jit(solution)/shard_map/all_to_all | solution.py:101
  484.9 4.3 multiply_convert_fusion.2
  489.2 47.4 %all-to-all-done.1 = bf16[1,256,2,30,128]{4,2,3,0,1:T(2,128)(2,1)} async-done(((bf16[1,256,2,30,128]{4,2,3,0,1:T(2,128)(2,1)}), bf16[1,256,2,30,128]{4,2,3,0,1:T(2,128)(2,1)}, u32[]{:S(2)}, u32[]{:S(2)}) %all-to-all-start.1) | async-done | bytes 3932192 | tf_op jit(solution)/shard_map/all_to_all | solution.py:101
  536.7 3.1 copy.59
  539.8 0.7 copy.60
  540.5 0.0 copy-start.1
  540.5 3.5 fusion.24
  544.0 0.0 copy-done.1
  (1 shorter events, 0.0 us)
Async XLA Ops:
  6.5 0.7 copy-start
  6.5 85.7 %all-gather.2.cloned.1.call-start = ((), (), s32[]{:S(2)}) async-start(), calls=%async_computation.2 | async-start | bytes 17694720 | tf_op jit(solution)/shard_map/all_gather | solution.py:43
  92.3 2.7 copy-start.2
  129.1 211.2 %all-to-all-start = ((bf16[3,16,2,480,128]{4,1,2,0,3:T(8,128)(2,1)}), bf16[3,16,2,480,128]{4,1,2,0,3:T(8,128)(2,1)}, u32[]{:S(2)}, u32[]{:S(2)}) async-start(bf16[3,16,2,480,128]{4,1,2,0,3:T(8,128)(2,1)} %copy.46), calls=%async_computation | async-start | bytes 23592960 | tf_op jit(solution)/shard_map/all_to_all | solution.py:58
  474.5 62.2 %all-to-all-start.1 = ((bf16[1,256,2,30,128]{4,2,3,0,1:T(2,128)(2,1)}), bf16[1,256,2,30,128]{4,2,3,0,1:T(2,128)(2,1)}, u32[]{:S(2)}, u32[]{:S(2)}) async-start(bf16[1,256,2,30,128]{4,2,3,0,1:T(2,128)(2,1)} %copy.58), calls=%async_computation.1 | async-start | bytes 7864320 | tf_op jit(solution)/shard_map/all_to_all | solution.py:101
  540.5 3.5 copy-start.1
Sparse Core Ops, SparseCore 0:
  9.0 83.1 all-gather.1
where the time goes:
time: 560 us; the launch traced here: 551 us
  local copies, waits for them, and re-layouts  297 us (53%)
  waiting for transfers between devices  154 us (28%)
  matrix products  33.2 us (6%)
  other arithmetic  30.8 us (6%)
  starting transfers between devices  17.8 us (3%)
  between operations  17.7 us (3%)
    convert_element_type x2, local copies, waits for them, and re-layouts, column_matrix(): jnp.stack([upper, lower], axis=1).reshape(2 * length, 2 * length)  97.8 us
    all_gather x1, waiting for transfers between devices, on_device(): shards = lax.all_gather(features, 'gop', axis=0, tiled=True)  76.1 us
    all_to_all x1, waiting for transfers between devices, on_device(): lax.all_to_all(back, 'row', split_axis=1, concat_axis=3, tiled=True)  47.4 us
    another operation x2, local copies, waits for them, and re-layouts, column_matrix(): jnp.stack([upper, lower], axis=1).reshape(2 * length, 2 * length)  44.4 us
    all_to_all x1, waiting for transfers between devices, on_device(): lax.all_to_all(done.astype(jnp.bfloat16).reshape(count, frames_in.shape[1...  30.2 us
    reshape x1, local copies, waits for them, and re-layouts, on_device(): done.astype(jnp.bfloat16)  27.6 us
    another operation x8, other arithmetic  27.5 us
    slice x1, local copies, waits for them, and re-layouts, on_device(): gain_real = filters[which_one, :, 0].astype(jnp.float32)  26.3 us
  transfers between devices with their start and end apart: 3, of which 3 were waited for; matrix products, arithmetic and copies ran while one was open for 33% of the time, Pallas kernels for 0%

commit v1 on v0

v1 whole, which is shorter than its diff:
```python
import math

import jax
import jax.numpy as jnp
from jax import lax
from jax.sharding import PartitionSpec as P


def row_table(length):
    across = jnp.arange(length, dtype=jnp.int32)
    phases = across[:, None] * across[None, :] % length
    angles = phases.astype(jnp.float32) * (2.0 * math.pi / length)
    factor = 1.0 / math.sqrt(length)
    return jnp.concatenate([jnp.cos(angles) * factor, -jnp.sin(angles) * factor], axis=1).astype(
        jnp.bfloat16
    )


def column_matrix(length, sign):
    across = jnp.arange(length, dtype=jnp.int32)
    phases = across[:, None] * across[None, :] % length
    angles = phases.astype(jnp.float32) * (2.0 * math.pi / length)
    factor = 1.0 / math.sqrt(length)
    cosine = jnp.cos(angles) * factor
    sine_part = sign * jnp.sin(angles) * factor
    upper = jnp.stack([cosine, -sine_part], axis=-1)
    lower = jnp.stack([sine_part, cosine], axis=-1)
    return jnp.stack([upper, lower], axis=1).reshape(2 * length, 2 * length).astype(jnp.bfloat16)


AXES = ("gop", "row")


def on_device(features, filters, anchors):
    frames = lax.psum(1, "gop")
    blocks = lax.psum(1, "row")
    _, hb, columns, chans = features.shape
    height = filters.shape[1]
    wb = columns // blocks
    cb = chans // frames
    me_gop = lax.axis_index("gop")

    forward_rows = row_table(columns)
    forward_cols = column_matrix(height, -1.0)
    forward_cols = forward_cols.reshape(height, 2, 2 * height).transpose(1, 0, 2).reshape(2 * height, 2 * height)
    inverse_cols = column_matrix(height, 1.0)
    inverse_cols = inverse_cols.reshape(2 * height, height, 2).transpose(0, 2, 1).reshape(2 * height, 2 * height)

    x = features[0]
    rowwise = jnp.einsum("hwc,wk->hkc", x, forward_rows, preferred_element_type=jnp.float32)
    rowwise = rowwise.astype(jnp.bfloat16)
    send = rowwise.reshape(hb, 2, blocks, wb, frames, cb).transpose(4, 2, 0, 1, 3, 5)
    send = send.reshape(frames * blocks, hb * 2, wb * cb)
    recv = lax.all_to_all(send, AXES, 0, 0, tiled=True)
    stacked = recv.reshape(frames, blocks * hb * 2, wb * cb)
    spectra = jnp.einsum("ab,fbn->fan", forward_cols, stacked, preferred_element_type=jnp.float32)
    spectra = spectra.astype(jnp.bfloat16).reshape(frames, 2, height, wb * cb)

    gains = filters.reshape(3, height, 2, wb, frames, cb)
    gains = lax.dynamic_index_in_dim(gains, me_gop, axis=4, keepdims=False)
    gains = gains.transpose(0, 2, 1, 3, 4).reshape(3, 2, height, wb * cb).astype(jnp.float32)

    first = jnp.take(spectra, anchors[:, 0], axis=0, mode="clip")
    second = jnp.take(spectra, anchors[:, 1], axis=0, mode="clip")
    sources = (spectra, first, second)
    real_part = jnp.zeros((frames, height, wb * cb), jnp.float32)
    imag_part = jnp.zeros((frames, height, wb * cb), jnp.float32)
    for which_one in range(3):
        source_real = sources[which_one][:, 0].astype(jnp.float32)
        source_imag = sources[which_one][:, 1].astype(jnp.float32)
        gain_real = gains[which_one, 0]
        gain_imag = gains[which_one, 1]
        real_part = real_part + gain_real * source_real - gain_imag * source_imag
        imag_part = imag_part + gain_real * source_imag + gain_imag * source_real
    mixed = jnp.stack([real_part, imag_part], axis=1).astype(jnp.bfloat16)
    mixed = mixed.reshape(frames, 2 * height, wb * cb)
    back = jnp.einsum("ab,fbn->fan", inverse_cols, mixed, preferred_element_type=jnp.float32)
    back = back.astype(jnp.bfloat16)
    send2 = back.reshape(frames * blocks, hb * 2, wb * cb)
    recv2 = lax.all_to_all(send2, AXES, 0, 0, tiled=True)
    recv2 = recv2.reshape(frames, blocks, hb, 2, wb, cb)
    table = forward_rows.reshape(columns, 2, blocks, wb)
    spatial = jnp.einsum("grhpkc,wprk->hwgc", recv2, table, preferred_element_type=jnp.float32)
    spatial = spatial.reshape(hb, columns, chans)
    out = (x.astype(jnp.float32) + spatial).astype(jnp.bfloat16)
    return out[None]


def solution(mesh):
    in_specs = (P("gop", "row", None, None), P(None, None, None, "row", None), P())
    out_specs = P("gop", "row", None, None)
    return jax.shard_map(
        on_device, mesh=mesh, in_specs=in_specs, out_specs=out_specs, check_vma=False
    )
```

time: 560 us -> 379 us (0.68)
  waiting for transfers between devices: 154 us -> 59.2 us
  local copies, waits for them, and re-layouts: 297 us -> 240 us
  between operations: 17.7 us -> 0.18 us
  other arithmetic: 30.8 us -> 24.9 us
    reshape x4 -> x6, local copies, waits for them, and re-layouts: 62 us -> 181 us  [the longest x2 91.3 us: on_device(): send = send.reshape(frames * blocks, hb * 2, wb * cb)]
    convert_element_type x2 -> x1, local copies, waits for them, and re-layouts: 97.8 us -> 0.2 us  [column_matrix(): jnp.stack([upper, lower], axis=1).reshape(2 * length, 2 * length)]
    all_gather x1 -> x0, waiting for transfers between devices: 76.1 us -> none  [on_device(): shards = lax.all_gather(features, 'gop', axis=0, tiled=True)]
    slice x9 -> x1, local copies, waits for them, and re-layouts: 75.8 us -> 0.01 us  [on_device(): first = jnp.take(spectra, anchors[:, 0], axis=0, mode='clip')]
    another operation x2 -> x3, local copies, waits for them, and re-layouts: 44.4 us -> 0.75 us  [column_matrix(): jnp.stack([upper, lower], axis=1).reshape(2 * length, 2 * length)]
    unnamed x6 -> x5, local copies, waits for them, and re-layouts: 0.03 us -> 29.7 us
    all_to_all x2, waiting for transfers between devices: 77.6 us -> 59.2 us  [the longest x1 46 us: on_device(): recv2 = lax.all_to_all(send2, AXES, 0, 0, tiled=True)]
    all_to_all x3 -> x0, local copies, waits for them, and re-layouts: 17.2 us -> none  [the longest x1 13.5 us: on_device(): lax.all_to_all(done.astype(jnp.bfloat16).reshape(count, frames_in.shape[1...]
  transfers between devices with their start and end apart: 3 -> 2, of which waited for: 3 -> 2; matrix products, arithmetic and copies ran while one was open for 33% -> 11% of each run, Pallas kernels for 0% -> 0%
where the time goes in v1:
time: 379 us; the launch traced here: 374 us
  local copies, waits for them, and re-layouts  240 us (63%)
  waiting for transfers between devices  59.2 us (16%)
  matrix products  31.8 us (8%)
  other arithmetic  24.9 us (7%)
  starting transfers between devices  17.8 us (5%)
    reshape x2, local copies, waits for them, and re-layouts, on_device(): send = send.reshape(frames * blocks, hb * 2, wb * cb)  91.3 us
    reshape x1, local copies, waits for them, and re-layouts, on_device(): rowwise.reshape(hb, 2, blocks, wb, frames, cb).transpose(4, 2, 0, 1, 3, 5)  46.7 us
    all_to_all x1, waiting for transfers between devices, on_device(): recv2 = lax.all_to_all(send2, AXES, 0, 0, tiled=True)  46 us
    reshape x1, local copies, waits for them, and re-layouts, on_device(): recv2 = recv2.reshape(frames, blocks, hb, 2, wb, cb)  35 us
    unnamed x5, local copies, waits for them, and re-layouts  29.7 us
    another operation x6, other arithmetic  19.1 us
    dot_general x1, matrix products, on_device(): jnp.einsum('grhpkc,wprk->hwgc', recv2, table, preferred_element_type=jnp....  17.1 us
    all_to_all x1, waiting for transfers between devices, on_device(): recv = lax.all_to_all(send, AXES, 0, 0, tiled=True)  13.3 us
  transfers between devices with their start and end apart: 2, of which 2 were waited for; matrix products, arithmetic and copies ran while one was open for 11% of the time, Pallas kernels for 0%

profile of v1, /device:TPU:0, one launch (start us, length us, event | category | flops | bytes accessed | tf_op | source)
XLA Modules:
  0.0 374.3 jit_solution(10053397787827208873)
XLA Ops:
  0.0 4.3 %multiply_convert_fusion.2 = (bf16[480,480]{0,1:T(8,128)(2,1)S(1)}, bf16[480,480]{0,1:T(8,128)(2,1)S(1)}) fusion(), kind=kLoop, calls=%fused_computation.59 | loop fusion | flops 3225600 | bytes 921600 | tf_op jit(solution)/shard_map/convert.22
  4.3 5.6 %convert_bitcast_fusion = bf16[16,960,128]{2,1,0:T(8,128)(2,1)} fusion(bf16[1,16,480,128]{3,2,1,0:T(8,128)(2,1)} %param.3, bf16[480,480]{0,1:T(8,128)(2,1)S(1)} %get-tuple-element.21, bf16[480,480]{0,1:T(8,128)(2,1)S(1)} %get-tuple-element.22), kind=kOutput, calls=%fused_computation.36 | convolution fusion | flops 1891246080 | bytes 6819840 | tf_op jit(solution)/shard_map/hwc,wk->hkc/dot_general | solution.py:50
  9.9 6.3 %copy.49 = bf16[16,960,128]{1,2,0:T(8,128)(2,1)} copy(bf16[16,960,128]{2,1,0:T(8,128)(2,1)} %convert_bitcast_fusion) | data formatting | bytes 7864320 | tf_op jit(solution)/shard_map/convert_element_type | solution.py:51
  16.2 46.7 %reshape.210 = bf16[16,2,16,30,8,16]{3,2,1,5,4,0:T(8,128)(2,1)} reshape(bf16[16,960,128]{1,2,0:T(8,128)(2,1)} %copy.49) | data formatting | bytes 7864320 | tf_op jit(solution)/shard_map/reshape | solution.py:52
  62.9 39.5 %copy.70 = bf16[8,16,16,2,30,16]{5,4,3,2,1,0:T(8,128)(2,1)} copy(bf16[8,16,16,2,30,16]{4,1,3,5,0,2:T(8,128)(2,1)} %bitcast.85) | data formatting | bytes 7864320 | tf_op jit(solution)/shard_map/reshape | solution.py:53
  102.4 51.8 %reshape.242 = bf16[128,32,480]{2,1,0:T(8,128)(2,1)} reshape(bf16[8,16,16,2,30,16]{5,4,3,2,1,0:T(8,128)(2,1)} %copy.70) | data formatting | bytes 7864320 | tf_op jit(solution)/shard_map/reshape | solution.py:53
  154.2 11.9 %all-to-all-start = ((bf16[128,32,480]{2,1,0:T(8,128)(2,1)}), bf16[128,32,480]{2,1,0:T(8,128)(2,1)}, u32[]{:S(2)}, u32[]{:S(2)}) async-start(bf16[128,32,480]{2,1,0:T(8,128)(2,1)} %reshape.242), calls=%async_computation | async-start | bytes 8388608 | tf_op jit(solution)/shard_map/all_to_all | solution.py:54
  166.1 1.0 multiply_convert_fusion.6
  167.1 1.0 negate_convert_fusion
  168.1 1.1 multiply_convert_fusion.4
  169.2 0.1 fusion.41
  169.3 0.2 copy.52
  169.5 0.1 stack.52
  169.6 0.2 copy.53
  169.8 0.1 stack.54
  169.9 0.1 maximum_bitcast_fusion.4
  170.0 1.0 copy.54
  171.0 0.0 copy-start.1
  171.0 29.7 %copy.48 = bf16[3,256,2,30,128]{1,4,3,2,0:T(8,128)(2,1)} copy(bf16[3,256,2,30,128]{4,2,3,1,0:T(2,128)(2,1)} %param.4) | data formatting | bytes 23592960 | tf_op args[1]
  200.7 0.1 pad_maximum_fusion
  200.7 0.5 copy.60
  201.3 0.2 convert_element_type.154
  201.5 0.0 copy-done.1
  201.5 1.8 bitcast_convert_fusion.1
  203.3 0.4 slice_bitcast_fusion.5
  203.7 13.3 %all-to-all-done = bf16[128,32,480]{2,1,0:T(8,128)(2,1)} async-done(((bf16[128,32,480]{2,1,0:T(8,128)(2,1)}), bf16[128,32,480]{2,1,0:T(8,128)(2,1)}, u32[]{:S(2)}, u32[]{:S(2)}) %all-to-all-start) | async-done | bytes 3932192 | tf_op jit(solution)/shard_map/all_to_all | solution.py:54
  217.0 4.9 %convolution_convert_fusion = bf16[8,480,512]{2,1,0:T(8,128)(2,1)S(1)} fusion(bf16[8,512,480]{2,1,0:T(8,128)(2,1)} %bitcast.11, bf16[512,512,1]{1,0,2:T(8,128)(2,1)} %bitcast.91), kind=kOutput, calls=%fused_computation.37 | convolution fusion | flops 2015232000 | bytes 8388608 | tf_op jit(solution)/shard_map/ab,fbn->fan/dot_general | solution.py:56
  221.8 2.3 copy.80
  224.1 4.9 %gather_fusion = bf16[8,2,256,480]{2,3,1,0:T(8,128)(2,1)} fusion(bf16[8,2,256,480]{2,3,1,0:T(8,128)(2,1)} %bitcast.82, s32[1024]{0:T(1024)S(1)} %get-tuple-element.28), kind=kCustom, calls=%fused_computation | custom fusion | bytes 7864352 | tf_op jit(solution)/shard_map/jit(_take)/gather | solution.py:63
  229.0 4.8 %gather_fusion.1 = bf16[8,2,256,480]{2,3,1,0:T(8,128)(2,1)} fusion(bf16[8,2,256,480]{2,3,1,0:T(8,128)(2,1)} %bitcast.83, s32[1024]{0:T(1024)S(1)} %get-tuple-element.27), kind=kCustom, calls=%fused_computation.1 | custom fusion | bytes 7864352 | tf_op jit(solution)/shard_map/jit(_take)/gather | solution.py:64
  233.7 6.7 %fusion.7 = (bf16[8,1,256,480]{2,3,1,0:T(8,128)(2,1)S(1)}, bf16[8,1,256,480]{2,3,1,0:T(8,128)(2,1)S(1)}) fusion(f32[256,480]{0,1:T(8,128)S(1)} %get-tuple-element.8, f32[256,480]{0,1:T(8,128)S(1)} %get-tuple-element.9, f32[256,480]{0,1:T(8,128)S(1)} %get-tuple-element.10, f32[256,480]{0,1:T(8,128)S(1)} %get-tuple-element.11, ...), kind=kLoop, calls=%fused_computation.22 | loop fusion | flops 29491200 | bytes 18677760 | tf_op jit(solution)/shard_map/convert.11
  240.4 4.2 %fusion.14 = bf16[8,512,480]{1,2,0:T(8,128)(2,1)} fusion(bf16[8,1,256,480]{2,3,1,0:T(8,128)(2,1)S(1)} %get-tuple-element.6, bf16[8,1,256,480]{2,3,1,0:T(8,128)(2,1)S(1)} %get-tuple-element.5, bf16[512,256,2]{1,0,2:T(8,128)(2,1)S(1)} %convert_element_type.154), kind=kOutput, calls=%fused_computation.29 | convolution fusion | flops 2017198080 | bytes 8388608 | tf_op jit(solution)/shard_map/ab,fbn->fan/dot_general | solution.py:77
  244.6 6.4 %copy.61 = bf16[8,512,480]{2,1,0:T(8,128)(2,1)} copy(bf16[8,512,480]{1,2,0:T(8,128)(2,1)} %fusion.14) | data formatting | bytes 7864320 | tf_op jit(solution)/shard_map/convert_element_type | solution.py:78
  251.0 5.9 %all-to-all-start.1 = ((bf16[128,32,480]{2,1,0:T(8,128)(2,1)}), bf16[128,32,480]{2,1,0:T(8,128)(2,1)}, u32[]{:S(2)}, u32[]{:S(2)}) async-start(bf16[128,32,480]{2,1,0:T(8,128)(2,1)} %bitcast.86), calls=%async_computation.1 | async-start | bytes 8388608 | tf_op jit(solution)/shard_map/all_to_all | solution.py:80
  257.0 5.1 %multiply_convert_fusion.1 = (bf16[480,1,16,30]{0,3,2,1:T(8,128)(2,1)S(1)}, bf16[480,1,16,30]{0,3,2,1:T(8,128)(2,1)S(1)}) fusion(s32[16,30]{1,0:T(8,128)S(1)} %multiply_add_fusion), kind=kLoop, calls=%fused_computation.49 | loop fusion | flops 3225600 | bytes 923520 | tf_op jit(solution)/shard_map/convert.23
  262.1 46.0 %all-to-all-done.1 = bf16[128,32,480]{2,1,0:T(8,128)(2,1)} async-done(((bf16[128,32,480]{2,1,0:T(8,128)(2,1)}), bf16[128,32,480]{2,1,0:T(8,128)(2,1)}, u32[]{:S(2)}, u32[]{:S(2)}) %all-to-all-start.1) | async-done | bytes 3932192 | tf_op jit(solution)/shard_map/all_to_all | solution.py:80
  308.0 35.0 %reshape.243 = bf16[8,16,16,2,30,16]{5,4,3,2,1,0:T(8,128)(2,1)} reshape(bf16[128,32,480]{2,1,0:T(8,128)(2,1)} %all-to-all-done.1) | data formatting | bytes 7864320 | tf_op jit(solution)/shard_map/reshape | solution.py:81
  343.0 17.1 %fusion.21 = f32[16,480,8,16]{1,3,0,2:T(8,128)} fusion(bf16[8,16,16,2,30,16]{5,4,3,2,1,0:T(8,128)(2,1)} %reshape.243, bf16[480,1,16,30]{0,3,2,1:T(8,128)(2,1)S(1)} %get-tuple-element.18, bf16[480,1,16,30]{0,3,2,1:T(8,128)(2,1)S(1)} %get-tuple-element.17), kind=kOutput, calls=%fused_computation.38 | convolution fusion | flops 1889280000 | bytes 8785920 | tf_op jit(solution)/shard_map/grhpkc,wprk->hwgc/dot_general | solution.py:83
  360.1 5.0 %copy.64 = f32[16,480,8,16]{1,3,2,0:T(8,128)} copy(f32[16,480,8,16]{1,3,0,2:T(8,128)} %fusion.21) | data formatting | bytes 7864320 | tf_op jit(solution)/shard_map/grhpkc,wprk->hwgc/transpose | solution.py:83
  365.1 0.0 copy-start
  365.1 5.4 %copy.65 = f32[1,16,480,128]{3,2,1,0:T(8,128)} copy(f32[1,16,480,128]{2,3,1,0:T(8,128)} %bitcast.87) | data formatting | bytes 7864320 | tf_op jit(solution)/shard_map/reshape | solution.py:84
  370.5 0.0 copy-done
  370.5 3.8 %add_convert_fusion = bf16[1,16,480,128]{3,2,1,0:T(8,128)(2,1)} fusion(f32[1,16,480,128]{3,2,1,0:T(8,128)} %copy.65, bf16[1,16,480,128]{3,2,1,0:T(8,128)(2,1)S(1)} %copy-done), kind=kLoop, calls=%fused_computation.35 | loop fusion | flops 2949120 | bytes 7864320 | tf_op jit(solution)/shard_map/convert_element_type | solution.py:85
  (3 shorter events, 0.0 us)
Async XLA Ops:
  154.2 62.8 %all-to-all-start = ((bf16[128,32,480]{2,1,0:T(8,128)(2,1)}), bf16[128,32,480]{2,1,0:T(8,128)(2,1)}, u32[]{:S(2)}, u32[]{:S(2)}) async-start(bf16[128,32,480]{2,1,0:T(8,128)(2,1)} %reshape.242), calls=%async_computation | async-start | bytes 8388608 | tf_op jit(solution)/shard_map/all_to_all | solution.py:54
  171.0 30.5 %copy-start.1 = (s32[8,2]{0,1:T(2,128)S(1)}, s32[8,2]{0,1:T(2,128)}, u32[]{:S(2)}) copy-start(s32[8,2]{0,1:T(2,128)} %param.5) | copy-start | bytes 196
  251.0 57.0 %all-to-all-start.1 = ((bf16[128,32,480]{2,1,0:T(8,128)(2,1)}), bf16[128,32,480]{2,1,0:T(8,128)(2,1)}, u32[]{:S(2)}, u32[]{:S(2)}) async-start(bf16[128,32,480]{2,1,0:T(8,128)(2,1)} %bitcast.86), calls=%async_computation.1 | async-start | bytes 8388608 | tf_op jit(solution)/shard_map/all_to_all | solution.py:80
  365.1 5.4 %copy-start = (bf16[1,16,480,128]{3,2,1,0:T(8,128)(2,1)S(1)}, bf16[1,16,480,128]{3,2,1,0:T(8,128)(2,1)}, u32[]{:S(2)}) copy-start(bf16[1,16,480,128]{3,2,1,0:T(8,128)(2,1)} %param.3) | copy-start | bytes 5898244

commit v2 on v1

v2 whole, which is shorter than its diff:
```python
import math

import jax
import jax.numpy as jnp
from jax import lax
from jax.sharding import PartitionSpec as P


def row_table(length):
    across = jnp.arange(length, dtype=jnp.int32)
    phases = across[:, None] * across[None, :] % length
    angles = phases.astype(jnp.float32) * (2.0 * math.pi / length)
    factor = 1.0 / math.sqrt(length)
    return jnp.concatenate([jnp.cos(angles) * factor, -jnp.sin(angles) * factor], axis=1).astype(
        jnp.bfloat16
    )


def column_matrix(length, sign):
    rows = lax.broadcasted_iota(jnp.int32, (2 * length, 2 * length), 0)
    cols = lax.broadcasted_iota(jnp.int32, (2 * length, 2 * length), 1)
    k, p = rows // 2, rows % 2
    h, q = cols // 2, cols % 2
    phases = k * h % length
    angles = phases.astype(jnp.float32) * (2.0 * math.pi / length)
    factor = 1.0 / math.sqrt(length)
    cosine = jnp.cos(angles) * factor
    sine_part = sign * jnp.sin(angles) * factor
    value = jnp.where(p == q, cosine, jnp.where(p == 0, -sine_part, sine_part))
    return value.astype(jnp.bfloat16)


def on_device(features, filters, anchors):
    frames = lax.psum(1, "gop")
    blocks = lax.psum(1, "row")
    _, hb, columns, chans = features.shape
    height = filters.shape[1]
    wb = columns // blocks
    kb = height // frames
    me_gop = lax.axis_index("gop")

    forward_rows = row_table(columns)
    split_table = forward_rows.reshape(columns, 2, columns)
    forward_cols = column_matrix(height, -1.0)
    inverse_cols = column_matrix(height, 1.0)

    x = features[0]
    rowwise = jnp.einsum("hwc,wk->hkc", x, forward_rows, preferred_element_type=jnp.float32)
    rowwise = rowwise.astype(jnp.bfloat16).reshape(hb, 2, columns, chans)
    slab = lax.all_to_all(rowwise, "row", 2, 0, tiled=True)
    spectra = jnp.dot(
        forward_cols, slab.reshape(2 * height, wb * chans), preferred_element_type=jnp.float32
    ).astype(jnp.bfloat16)
    spectra = spectra.reshape(frames, kb, 2, wb, chans)
    every = lax.all_to_all(spectra, "gop", 0, 0, tiled=True)

    gains = lax.dynamic_slice_in_dim(filters, me_gop * kb, kb, axis=1).astype(jnp.float32)
    first = jnp.take(every, anchors[:, 0], axis=0, mode="clip")
    second = jnp.take(every, anchors[:, 1], axis=0, mode="clip")
    sources = (every, first, second)
    real_part = jnp.zeros((frames, kb, wb, chans), jnp.float32)
    imag_part = jnp.zeros((frames, kb, wb, chans), jnp.float32)
    for which_one in range(3):
        source_real = sources[which_one][:, :, 0].astype(jnp.float32)
        source_imag = sources[which_one][:, :, 1].astype(jnp.float32)
        gain_real = gains[which_one, :, 0]
        gain_imag = gains[which_one, :, 1]
        real_part = real_part + gain_real * source_real - gain_imag * source_imag
        imag_part = imag_part + gain_real * source_imag + gain_imag * source_real
    mixed = jnp.stack([real_part, imag_part], axis=2).astype(jnp.bfloat16)
    mine = lax.all_to_all(mixed, "gop", 0, 0, tiled=True)
    back = jnp.dot(
        inverse_cols, mine.reshape(2 * height, wb * chans), preferred_element_type=jnp.float32
    ).astype(jnp.bfloat16)
    back = back.reshape(height, 2, wb, chans)
    rows_back = lax.all_to_all(back, "row", 0, 2, tiled=True)
    spatial = jnp.einsum(
        "hpkc,wpk->hwc", rows_back, split_table, preferred_element_type=jnp.float32
    )
    out = (x.astype(jnp.float32) + spatial).astype(jnp.bfloat16)
    return out[None]


def solution(mesh):
    in_specs = (P("gop", "row", None, None), P(None, None, None, "row", None), P())
    out_specs = P("gop", "row", None, None)
    return jax.shard_map(
        on_device, mesh=mesh, in_specs=in_specs, out_specs=out_specs, check_vma=False
    )
```

time: 379 us -> 327 us (0.86)
  the two profiles are of different devices: /device:TPU:0 before, /device:TPU:92 now
where the time goes in v2:
time: 327 us; the launch traced here: 326 us
  waiting for transfers between devices  159 us (49%)
  local copies, waits for them, and re-layouts  56.4 us (17%)
  blocking collectives  49.9 us (15%)
  matrix products  25.4 us (8%)
  starting transfers between devices  19.1 us (6%)
  other arithmetic  15.9 us (5%)
    all_to_all x1, waiting for transfers between devices, on_device(): slab = lax.all_to_all(rowwise, 'row', 2, 0, tiled=True)  61.2 us
    all_to_all x1, waiting for transfers between devices, on_device(): rows_back = lax.all_to_all(back, 'row', 0, 2, tiled=True)  57.3 us
    all_to_all x1, blocking collectives, on_device(): mine = lax.all_to_all(mixed, 'gop', 0, 0, tiled=True)  49.9 us
    all_to_all x1, waiting for transfers between devices, on_device(): every = lax.all_to_all(spectra, 'gop', 0, 0, tiled=True)  40.7 us
    reshape x2, local copies, waits for them, and re-layouts, on_device(): back = back.reshape(height, 2, wb, chans)  15.3 us
    another operation x3, other arithmetic  15.1 us
    reshape x2, local copies, waits for them, and re-layouts, on_device(): spectra = spectra.reshape(frames, kb, 2, wb, chans)  13.9 us
    dot_general x1, matrix products, on_device(): jnp.dot(forward_cols, slab.reshape(2 * height, wb * chans), preferred_ele...  9.1 us
  transfers between devices with their start and end apart: 3, of which 3 were waited for; matrix products, arithmetic and copies ran while one was open for 2% of the time, Pallas kernels for 0%

profile of v2, /device:TPU:92, one launch (start us, length us, event | category | flops | bytes accessed | tf_op | source)
XLA Modules:
  0.0 326.0 jit_solution(10704506809246923714)
XLA Ops:
  0.0 4.3 %multiply_convert_fusion = (bf16[480,480]{0,1:T(8,128)(2,1)S(1)}, bf16[480,480]{0,1:T(8,128)(2,1)S(1)}) fusion(), kind=kLoop, calls=%fused_computation.68 | loop fusion | flops 3225600 | bytes 921600 | tf_op jit(solution)/shard_map/convert.3
  4.3 3.7 %convolution_convert_fusion.2 = bf16[960,16,128]{2,0,1:T(8,128)(2,1)S(1)} fusion(bf16[1,16,480,128]{3,2,1,0:T(8,128)(2,1)} %param.3, bf16[480,480]{0,1:T(8,128)(2,1)S(1)} %get-tuple-element.15, bf16[480,480]{0,1:T(8,128)(2,1)S(1)} %get-tuple-element.16), kind=kOutput, calls=%fused_computation.37 | convolution fusion | flops 1891246080 | bytes 6819840 | tf_op jit(solution)/shard_map/hwc,wk->hkc/dot_general | solution.py:48
  8.0 4.4 %copy.25 = bf16[16,2,480,128]{3,0,1,2:T(8,128)(2,1)} copy(bf16[16,2,480,128]{3,2,1,0:T(8,128)(2,1)S(1)} %bitcast.61) | data formatting | bytes 7864320 | tf_op jit(solution)/shard_map/reshape | solution.py:49
  12.4 7.1 %all-to-all-start = ((bf16[16,2,480,128]{3,0,1,2:T(8,128)(2,1)}), bf16[16,2,480,128]{3,0,1,2:T(8,128)(2,1)}, u32[]{:S(2)}, u32[]{:S(2)}) async-start(bf16[16,2,480,128]{3,0,1,2:T(8,128)(2,1)} %copy.25), calls=%async_computation | async-start | bytes 7864320 | tf_op jit(solution)/shard_map/all_to_all | solution.py:50
  19.6 61.2 %all-to-all-done = bf16[16,2,480,128]{3,0,1,2:T(8,128)(2,1)} async-done(((bf16[16,2,480,128]{3,0,1,2:T(8,128)(2,1)}), bf16[16,2,480,128]{3,0,1,2:T(8,128)(2,1)}, u32[]{:S(2)}, u32[]{:S(2)}) %all-to-all-start) | async-done | bytes 3932192 | tf_op jit(solution)/shard_map/all_to_all | solution.py:50
  80.8 3.8 %copy.27 = bf16[16,16,2,30,128]{4,3,2,1,0:T(8,128)(2,1)S(1)} copy(bf16[16,16,2,30,128]{4,1,2,3,0:T(8,128)(2,1)} %bitcast.8) | data formatting | bytes 7864320 | tf_op jit(solution)/shard_map/all_to_all | solution.py:50
  84.5 9.1 %convolution_convert_fusion.1 = bf16[512,3840]{1,0:T(8,128)(2,1)} fusion(bf16[64,8,30,128]{3,2,1,0:T(8,128)(2,1)S(1)} %bitcast.59, s32[512]{0:T(512)S(1)} %get-tuple-element.18, s32[512]{0:T(512)S(1)} %get-tuple-element.19, pred[512]{0:T(512)(128)(4,1)S(1)} %get-tuple-element.22, s32[512]{0:T(512)S(1)} %get-tuple-element.17, s32[512]{0:T(512)S(1)} %get-tuple-element.20, ...), kind=kOutput, calls=%fused_computation.3 | convolution fusion | flops 2022047744 | bytes 7873536 | tf_op jit(solution)/shard_map/dot_general | solution.py:51
  93.6 7.2 %reshape.63 = bf16[8,32,2,30,128]{4,3,2,1,0:T(8,128)(2,1)} reshape(bf16[512,3840]{1,0:T(8,128)(2,1)} %convolution_convert_fusion.1) | data formatting | bytes 7864320 | tf_op jit(solution)/shard_map/reshape | solution.py:54
  100.9 6.6 %copy.28 = bf16[8,32,2,30,128]{4,1,3,2,0:T(8,128)(2,1)} copy(bf16[8,32,2,30,128]{4,3,2,1,0:T(8,128)(2,1)} %reshape.63) | data formatting | bytes 7864320 | tf_op jit(solution)/shard_map/reshape | solution.py:54
  107.5 0.0 copy-start
  107.5 5.0 %all-to-all-start.1 = ((bf16[8,32,2,30,128]{4,1,3,2,0:T(8,128)(2,1)}), bf16[8,32,2,30,128]{4,1,3,2,0:T(8,128)(2,1)}, u32[]{:S(2)}, u32[]{:S(2)}) async-start(bf16[8,32,2,30,128]{4,1,3,2,0:T(8,128)(2,1)} %copy.28), calls=%async_computation.1 | async-start | bytes 7864320 | tf_op jit(solution)/shard_map/all_to_all | solution.py:55
  112.6 0.0 copy-done
  112.6 2.4 constant_dynamic-slice_fusion
  115.0 0.4 copy_convert_fusion
  115.4 0.3 slice_bitcast_fusion.5
  115.7 40.7 %all-to-all-done.1 = bf16[8,32,2,30,128]{4,1,3,2,0:T(8,128)(2,1)} async-done(((bf16[8,32,2,30,128]{4,1,3,2,0:T(8,128)(2,1)}), bf16[8,32,2,30,128]{4,1,3,2,0:T(8,128)(2,1)}, u32[]{:S(2)}, u32[]{:S(2)}) %all-to-all-start.1) | async-done | bytes 3932192 | tf_op jit(solution)/shard_map/all_to_all | solution.py:55
  156.4 5.1 %gather_fusion = bf16[8,32,2,30,128]{4,1,3,2,0:T(8,128)(2,1)} fusion(bf16[8,32,2,30,128]{4,1,3,2,0:T(8,128)(2,1)} %all-to-all-done.1, s32[1024]{0:T(1024)S(1)} %get-tuple-element.24), kind=kCustom, calls=%fused_computation | custom fusion | bytes 7864352 | tf_op jit(solution)/shard_map/jit(_take)/gather | solution.py:58
  161.5 5.0 %gather_fusion.1 = bf16[8,32,2,30,128]{4,1,3,2,0:T(8,128)(2,1)} fusion(bf16[8,32,2,30,128]{4,1,3,2,0:T(8,128)(2,1)} %all-to-all-done.1, s32[1024]{0:T(1024)S(1)} %get-tuple-element.23), kind=kCustom, calls=%fused_computation.1 | custom fusion | bytes 7864352 | tf_op jit(solution)/shard_map/jit(_take)/gather | solution.py:59
  166.5 6.6 %fusion.5 = (bf16[8,32,1,30,128]{4,1,3,2,0:T(8,128)(2,1)S(1)}, bf16[8,32,1,30,128]{4,1,3,2,0:T(8,128)(2,1)S(1)}) fusion(f32[32,30,128]{2,0,1:T(8,128)S(1)} %get-tuple-element.8, f32[32,30,128]{2,0,1:T(8,128)S(1)} %get-tuple-element.9, f32[32,30,128]{2,0,1:T(8,128)S(1)} %get-tuple-element.10, f32[32,30,128]{2,0,1:T(8,128)S(1)} %get-tuple-element.11, ...), kind=kLoop, calls=%fused_computation.21 | loop fusion | flops 29491200 | bytes 18677760 | tf_op jit(solution)/shard_map/convert
  173.1 0.4 pad_maximum_fusion
  173.5 49.9 %all_to_all.43 = bf16[8,32,2,30,128]{4,1,3,2,0:T(8,128)(2,1)S(1)} all-to-all(bf16[8,32,2,30,128]{4,1,3,2,0:T(8,128)(2,1)S(1)} %pad_maximum_fusion), channel_id=1, replica_groups=mesh['gop'=8,'row'=16] {'gop'}, dimensions={0} | all-to-all | bytes 7864320 | tf_op jit(solution)/shard_map/all_to_all | solution.py:71
  223.4 1.6 copy.29
  224.9 9.1 %convolution_convert_fusion = bf16[512,3840]{1,0:T(8,128)(2,1)} fusion(bf16[64,8,30,128]{3,2,1,0:T(8,128)(2,1)S(1)} %bitcast.58, s32[512]{0:T(512)S(1)} %get-tuple-element.18, s32[512]{0:T(512)S(1)} %get-tuple-element.19, pred[512]{0:T(512)(128)(4,1)S(1)} %get-tuple-element.22, s32[512]{0:T(512)S(1)} %get-tuple-element.17, s32[512]{0:T(512)S(1)} %get-tuple-element.20, ...), kind=kOutput, calls=%fused_computation.2 | convolution fusion | flops 2022047744 | bytes 7873536 | tf_op jit(solution)/shard_map/dot_general | solution.py:72
  234.0 7.2 %reshape.65 = bf16[256,2,30,128]{3,2,1,0:T(8,128)(2,1)} reshape(bf16[512,3840]{1,0:T(8,128)(2,1)} %convolution_convert_fusion) | data formatting | bytes 7864320 | tf_op jit(solution)/shard_map/reshape | solution.py:75
  241.2 8.1 %copy.30 = bf16[256,2,30,128]{3,1,2,0:T(2,128)(2,1)} copy(bf16[256,2,30,128]{3,2,1,0:T(8,128)(2,1)} %reshape.65) | data formatting | bytes 7864320 | tf_op jit(solution)/shard_map/reshape | solution.py:75
  249.3 6.9 %all-to-all-start.3 = ((bf16[256,2,30,128]{3,1,2,0:T(2,128)(2,1)}), bf16[256,2,30,128]{3,1,2,0:T(2,128)(2,1)}, u32[]{:S(2)}, u32[]{:S(2)}) async-start(bf16[256,2,30,128]{3,1,2,0:T(2,128)(2,1)} %copy.30), calls=%async_computation.3 | async-start | bytes 7864320 | tf_op jit(solution)/shard_map/all_to_all | solution.py:76
  256.3 4.3 %multiply_convert_fusion.2 = (bf16[480,1,480]{2,0,1:T(8,128)(2,1)S(1)}, bf16[480,1,480]{2,0,1:T(8,128)(2,1)S(1)}) fusion(), kind=kLoop, calls=%fused_computation.73 | loop fusion | flops 3225600 | bytes 921600 | tf_op jit(solution)/shard_map/convert.5
  260.6 57.3 %all-to-all-done.3 = bf16[256,2,30,128]{3,1,2,0:T(2,128)(2,1)} async-done(((bf16[256,2,30,128]{3,1,2,0:T(2,128)(2,1)}), bf16[256,2,30,128]{3,1,2,0:T(2,128)(2,1)}, u32[]{:S(2)}, u32[]{:S(2)}) %all-to-all-start.3) | async-done | bytes 3932192 | tf_op jit(solution)/shard_map/all_to_all | solution.py:76
  317.8 3.1 copy.31
  321.0 0.0 copy-start.1
  321.0 0.7 copy.32
  321.6 0.9 copy-done.1
  322.5 3.5 %fusion.19 = bf16[1,16,480,128]{3,2,1,0:T(8,128)(2,1)} fusion(bf16[1,16,480,128]{3,2,1,0:T(8,128)(2,1)S(1)} %copy-done.1, bf16[16,2,480,128]{3,0,2,1:T(8,128)(2,1)S(1)} %bitcast.60, bf16[480,1,480]{2,0,1:T(8,128)(2,1)S(1)} %get-tuple-element.25, bf16[480,1,480]{2,0,1:T(8,128)(2,1)S(1)} %get-tuple-element.26), kind=kOutput, calls=%fused_computation.38 | convolution fusion | flops 1892229120 | bytes 8785920 | tf_op jit(solution)/shard_map/hpkc,wpk->hwc/dot_general | solution.py:77
  (5 shorter events, 0.0 us)
Async XLA Ops:
  12.4 68.3 %all-to-all-start = ((bf16[16,2,480,128]{3,0,1,2:T(8,128)(2,1)}), bf16[16,2,480,128]{3,0,1,2:T(8,128)(2,1)}, u32[]{:S(2)}, u32[]{:S(2)}) async-start(bf16[16,2,480,128]{3,0,1,2:T(8,128)(2,1)} %copy.25), calls=%async_computation | async-start | bytes 7864320 | tf_op jit(solution)/shard_map/all_to_all | solution.py:50
  107.5 5.1 %copy-start = (s32[8,2]{0,1:T(2,128)S(1)}, s32[8,2]{0,1:T(2,128)}, u32[]{:S(2)}) copy-start(s32[8,2]{0,1:T(2,128)} %param.5) | copy-start | bytes 196
  107.5 48.9 %all-to-all-start.1 = ((bf16[8,32,2,30,128]{4,1,3,2,0:T(8,128)(2,1)}), bf16[8,32,2,30,128]{4,1,3,2,0:T(8,128)(2,1)}, u32[]{:S(2)}, u32[]{:S(2)}) async-start(bf16[8,32,2,30,128]{4,1,3,2,0:T(8,128)(2,1)} %copy.28), calls=%async_computation.1 | async-start | bytes 7864320 | tf_op jit(solution)/shard_map/all_to_all | solution.py:55
  249.3 68.5 %all-to-all-start.3 = ((bf16[256,2,30,128]{3,1,2,0:T(2,128)(2,1)}), bf16[256,2,30,128]{3,1,2,0:T(2,128)(2,1)}, u32[]{:S(2)}, u32[]{:S(2)}) async-start(bf16[256,2,30,128]{3,1,2,0:T(2,128)(2,1)} %copy.30), calls=%async_computation.3 | async-start | bytes 7864320 | tf_op jit(solution)/shard_map/all_to_all | solution.py:76
  321.0 1.6 copy-start.1

commit v3 on v2

v3 whole, which is shorter than its diff:
```python
import math

import jax
import jax.numpy as jnp
from jax import lax
from jax.sharding import PartitionSpec as P


def row_table(length):
    across = jnp.arange(length, dtype=jnp.int32)
    phases = across[:, None] * across[None, :] % length
    angles = phases.astype(jnp.float32) * (2.0 * math.pi / length)
    factor = 1.0 / math.sqrt(length)
    return jnp.concatenate([jnp.cos(angles) * factor, -jnp.sin(angles) * factor], axis=1).astype(
        jnp.bfloat16
    )


def column_matrix(length, sign, row_of, col_of):
    rows = lax.broadcasted_iota(jnp.int32, (2 * length, 2 * length), 0)
    cols = lax.broadcasted_iota(jnp.int32, (2 * length, 2 * length), 1)
    k, p = row_of(rows)
    h, q = col_of(cols)
    phases = k * h % length
    angles = phases.astype(jnp.float32) * (2.0 * math.pi / length)
    factor = 1.0 / math.sqrt(length)
    cosine = jnp.cos(angles) * factor
    sine_part = sign * jnp.sin(angles) * factor
    value = jnp.where(p == q, cosine, jnp.where(p == 0, -sine_part, sine_part))
    return value.astype(jnp.bfloat16)


def interleaved(index):
    return index // 2, index % 2


def blocked(kb):
    def split(index):
        blk, rest = index // (2 * kb), index % (2 * kb)
        return blk * kb + rest % kb, rest // kb

    return split


def on_device(features, filters, anchors):
    frames = lax.psum(1, "gop")
    blocks = lax.psum(1, "row")
    _, hb, columns, chans = features.shape
    height = filters.shape[1]
    wb = columns // blocks
    kb = height // frames
    lanes = wb * chans
    me_gop = lax.axis_index("gop")

    forward_rows = row_table(columns)
    forward_cols = column_matrix(height, -1.0, blocked(kb), interleaved)
    inverse_cols = column_matrix(height, 1.0, interleaved, blocked(kb))

    x = features[0]
    rowwise = jnp.einsum("hwc,wk->hkc", x, forward_rows, preferred_element_type=jnp.float32)
    rowwise = rowwise.astype(jnp.bfloat16).reshape(hb, 2, columns, chans)
    slab = lax.all_to_all(rowwise, "row", 2, 0, tiled=True)
    spectra = jnp.dot(
        forward_cols, slab.reshape(2 * height, lanes), preferred_element_type=jnp.float32
    ).astype(jnp.bfloat16)
    spectra = spectra.reshape(frames, 2 * kb, lanes)
    every = lax.all_to_all(spectra, "gop", 0, 0, tiled=True)
    every = every.reshape(frames, 2, kb, lanes)

    gains = lax.dynamic_slice_in_dim(filters, me_gop * kb, kb, axis=1)
    gains = gains.transpose(0, 2, 1, 3, 4).reshape(3, 2, kb, lanes).astype(jnp.float32)
    outs = []
    for frame in range(frames):
        sources = (
            every[frame],
            lax.dynamic_index_in_dim(every, anchors[frame, 0], 0, keepdims=False),
            lax.dynamic_index_in_dim(every, anchors[frame, 1], 0, keepdims=False),
        )
        real_part = jnp.zeros((kb, lanes), jnp.float32)
        imag_part = jnp.zeros((kb, lanes), jnp.float32)
        for which_one in range(3):
            source_real = sources[which_one][0].astype(jnp.float32)
            source_imag = sources[which_one][1].astype(jnp.float32)
            gain_real = gains[which_one, 0]
            gain_imag = gains[which_one, 1]
            real_part = real_part + gain_real * source_real - gain_imag * source_imag
            imag_part = imag_part + gain_real * source_imag + gain_imag * source_real
        outs.append(jnp.stack([real_part, imag_part]))
    mixed = jnp.stack(outs).astype(jnp.bfloat16).reshape(frames, 2 * kb, lanes)
    mine = lax.all_to_all(mixed, "gop", 0, 0, tiled=True)
    back = jnp.dot(
        inverse_cols, mine.reshape(2 * height, lanes), preferred_element_type=jnp.float32
    ).astype(jnp.bfloat16)
    back = back.reshape(blocks, 2 * hb, lanes)
    rows_back = lax.all_to_all(back, "row", 0, 0, tiled=True)
    rows_back = rows_back.reshape(blocks, hb, 2, wb, chans)
    table = forward_rows.reshape(columns, 2, blocks, wb)
    spatial = jnp.einsum(
        "rhpkc,wprk->hwc", rows_back, table, preferred_element_type=jnp.float32
    )
    out = (x.astype(jnp.float32) + spatial).astype(jnp.bfloat16)
    return out[None]


def solution(mesh):
    in_specs = (P("gop", "row", None, None), P(None, None, None, "row", None), P())
    out_specs = P("gop", "row", None, None)
    return jax.shard_map(
        on_device, mesh=mesh, in_specs=in_specs, out_specs=out_specs, check_vma=False
    )
```

time: 327 us -> 316 us (0.966)
  waiting for transfers between devices: 159 us -> 123 us
  local copies, waits for them, and re-layouts: 56.4 us -> 21.3 us
  between operations: 0.13 us -> 31 us
  other arithmetic: 15.9 us -> 40.2 us
  matrix products: 25.4 us -> 30 us
    all_to_all x1, waiting for transfers between devices: 40.7 us -> 4.97 us  [on_device(): every = lax.all_to_all(spectra, 'gop', 0, 0, tiled=True)]
    another operation x4 -> x26, other arithmetic: 15.5 us -> 37.7 us
    reshape x4 -> x1, local copies, waits for them, and re-layouts: 29.2 us -> 7.22 us  [on_device(): rows_back = rows_back.reshape(blocks, hb, 2, wb, chans)]
    gather x2 -> x0, local copies, waits for them, and re-layouts: 10.1 us -> none  [the longest x1 5.12 us: on_device(): first = jnp.take(every, anchors[:, 0], axis=0, mode='clip')]
    all_to_all x3 -> x0, local copies, waits for them, and re-layouts: 5.33 us -> none  [the longest x2 3.77 us: on_device(): rows_back = lax.all_to_all(back, 'row', 0, 2, tiled=True)]
    convert_element_type x0 -> x2, local copies, waits for them, and re-layouts: none -> 4.97 us  [on_device(): gains.transpose(0, 2, 1, 3, 4).reshape(3, 2, kb, lanes).astype(jnp.float32)]
    dot_general x3, matrix products: 21.7 us -> 26.3 us  [the longest x1 11.3 us: on_device(): jnp.dot(inverse_cols, mine.reshape(2 * height, lanes), preferred_element_...]
  transfers between devices with their start and end apart: 3 -> 3, of which waited for: 3 -> 3; matrix products, arithmetic and copies ran while one was open for 2% -> 4% of each run, Pallas kernels for 0% -> 0%
where the time goes in v3:
time: 316 us; the launch traced here: 314 us
  waiting for transfers between devices  123 us (39%)
  blocking collectives  49.9 us (16%)
  other arithmetic  40.2 us (13%)
  between operations  31 us (10%)
  matrix products  30 us (9%)
  local copies, waits for them, and re-layouts  21.3 us (7%)
  starting transfers between devices  19.1 us (6%)
    all_to_all x1, waiting for transfers between devices, on_device(): slab = lax.all_to_all(rowwise, 'row', 2, 0, tiled=True)  61.2 us
    all_to_all x1, waiting for transfers between devices, on_device(): rows_back = lax.all_to_all(back, 'row', 0, 0, tiled=True)  56.4 us
    all_to_all x1, blocking collectives, on_device(): mine = lax.all_to_all(mixed, 'gop', 0, 0, tiled=True)  49.9 us
    another operation x18, other arithmetic  37.4 us
    dot_general x1, matrix products, on_device(): jnp.dot(inverse_cols, mine.reshape(2 * height, lanes), preferred_element_...  11.3 us
    dot_general x1, matrix products, on_device(): jnp.dot(forward_cols, slab.reshape(2 * height, lanes), preferred_element_...  9.24 us
    reshape x1, local copies, waits for them, and re-layouts, on_device(): rows_back = rows_back.reshape(blocks, hb, 2, wb, chans)  7.22 us
    all_to_all x1, starting transfers between devices, on_device(): slab = lax.all_to_all(rowwise, 'row', 2, 0, tiled=True)  7.11 us
  transfers between devices with their start and end apart: 3, of which 3 were waited for; matrix products, arithmetic and copies ran while one was open for 4% of the time, Pallas kernels for 0%

profile of v3, /device:TPU:92, one launch (start us, length us, event | category | flops | bytes accessed | tf_op | source)
XLA Modules:
  0.0 314.1 jit_solution(2204209579282728914)
XLA Ops:
  0.0 4.3 %multiply_convert_fusion.2 = (bf16[480,480]{0,1:T(8,128)(2,1)S(1)}, bf16[480,480]{0,1:T(8,128)(2,1)S(1)}) fusion(), kind=kLoop, calls=%fused_computation.79 | loop fusion | flops 3225600 | bytes 921600 | tf_op jit(solution)/shard_map/convert.35
  4.3 3.7 %convolution_convert_fusion.2 = bf16[960,16,128]{2,0,1:T(8,128)(2,1)S(1)} fusion(bf16[1,16,480,128]{3,2,1,0:T(8,128)(2,1)} %param.3, bf16[480,480]{0,1:T(8,128)(2,1)S(1)} %get-tuple-element.23, bf16[480,480]{0,1:T(8,128)(2,1)S(1)} %get-tuple-element.24), kind=kOutput, calls=%fused_computation.9 | convolution fusion | flops 1891246080 | bytes 6819840 | tf_op jit(solution)/shard_map/hwc,wk->hkc/dot_general | solution.py:60
  8.0 4.4 %copy.10 = bf16[16,2,480,128]{3,0,1,2:T(8,128)(2,1)} copy(bf16[16,2,480,128]{3,2,1,0:T(8,128)(2,1)S(1)} %bitcast.412) | data formatting | bytes 7864320 | tf_op jit(solution)/shard_map/reshape | solution.py:61
  12.4 7.1 %all-to-all-start = ((bf16[16,2,480,128]{3,0,1,2:T(8,128)(2,1)}), bf16[16,2,480,128]{3,0,1,2:T(8,128)(2,1)}, u32[]{:S(2)}, u32[]{:S(2)}) async-start(bf16[16,2,480,128]{3,0,1,2:T(8,128)(2,1)} %copy.10), calls=%async_computation | async-start | bytes 7864320 | tf_op jit(solution)/shard_map/all_to_all | solution.py:62
  19.6 61.2 %all-to-all-done = bf16[16,2,480,128]{3,0,1,2:T(8,128)(2,1)} async-done(((bf16[16,2,480,128]{3,0,1,2:T(8,128)(2,1)}), bf16[16,2,480,128]{3,0,1,2:T(8,128)(2,1)}, u32[]{:S(2)}, u32[]{:S(2)}) %all-to-all-start) | async-done | bytes 3932192 | tf_op jit(solution)/shard_map/all_to_all | solution.py:62
  80.8 3.8 %copy.12 = bf16[16,16,2,30,128]{4,3,2,1,0:T(8,128)(2,1)S(1)} copy(bf16[16,16,2,30,128]{4,1,2,3,0:T(8,128)(2,1)} %bitcast.10) | data formatting | bytes 7864320 | tf_op jit(solution)/shard_map/all_to_all | solution.py:62
  84.5 9.2 %convolution_convert_fusion.1 = bf16[512,3840]{1,0:T(8,128)(2,1)} fusion(bf16[64,8,30,128]{3,2,1,0:T(8,128)(2,1)S(1)} %bitcast.408, s32[512]{0:T(512)S(1)} %get-tuple-element.29, s32[512]{0:T(512)S(1)} %get-tuple-element.36, s32[512]{0:T(512)S(1)} %get-tuple-element.31, s32[512]{0:T(512)S(1)} %get-tuple-element.35, s32[512]{0:T(512)S(1)} %get-tuple-element.30, ...), kind=kOutput, calls=%fused_computation.1 | convolution fusion | flops 2027552768 | bytes 7882752 | tf_op jit(solution)/shard_map/dot_general | solution.py:63
  93.8 0.0 copy-start
  93.8 5.0 %all-to-all-start.1 = ((bf16[8,64,3840]{2,1,0:T(8,128)(2,1)}), bf16[8,64,3840]{2,1,0:T(8,128)(2,1)}, u32[]{:S(2)}, u32[]{:S(2)}) async-start(bf16[8,64,3840]{2,1,0:T(8,128)(2,1)} %bitcast.409), calls=%async_computation.1 | async-start | bytes 7864320 | tf_op jit(solution)/shard_map/all_to_all | solution.py:67
  98.8 0.0 copy-done
  98.8 0.7 fusion.288
  120.0 2.4 convert_bitcast_fusion
  122.4 2.2 copy.9
  124.6 2.8 reshape.1436
  137.7 5.0 %all-to-all-done.1 = bf16[8,64,3840]{2,1,0:T(8,128)(2,1)} async-done(((bf16[8,64,3840]{2,1,0:T(8,128)(2,1)}), bf16[8,64,3840]{2,1,0:T(8,128)(2,1)}, u32[]{:S(2)}, u32[]{:S(2)}) %all-to-all-start.1) | async-done | bytes 3932192 | tf_op jit(solution)/shard_map/all_to_all | solution.py:67
  142.6 1.7 fusion.99
  144.4 1.8 fusion.105
  146.2 1.8 fusion.239
  148.0 1.8 fusion.245
  149.8 1.8 fusion.219
  151.6 1.8 fusion.225
  153.4 1.8 fusion.199
  155.1 1.8 fusion.205
  156.9 1.8 fusion.179
  158.7 1.8 fusion.185
  160.5 1.8 fusion.159
  162.2 1.8 fusion.165
  164.1 1.8 fusion.139
  165.8 1.8 fusion.145
  167.6 1.8 fusion.119
  169.4 1.8 fusion.125
  171.5 49.9 %all_to_all.30 = bf16[8,64,3840]{2,1,0:T(8,128)(2,1)S(1)} all-to-all(bf16[8,64,3840]{2,1,0:T(8,128)(2,1)S(1)} %bitcast_dynamic-update-slice_fusion), channel_id=1, replica_groups=mesh['gop'=8,'row'=16] {'gop'}, dimensions={0} | all-to-all | bytes 7864320 | tf_op jit(solution)/shard_map/all_to_all | solution.py:90
  221.4 11.3 %convolution_convert_fusion = bf16[512,3840]{1,0:T(8,128)(2,1)} fusion(bf16[512,3840]{1,0:T(8,128)(2,1)S(1)} %bitcast.411, s32[512]{0:T(512)S(1)} %get-tuple-element.31, s32[512]{0:T(512)S(1)} %get-tuple-element.35, s32[512]{0:T(512)S(1)} %get-tuple-element.29, s32[512]{0:T(512)S(1)} %get-tuple-element.36, s32[512]{0:T(512)S(1)} %get-tuple-element.32, ...), kind=kOutput, calls=%fused_computation | convolution fusion | flops 2027552768 | bytes 7882752 | tf_op jit(solution)/shard_map/dot_general | solution.py:91
  232.7 6.9 %all-to-all-start.3 = ((bf16[16,32,3840]{2,1,0:T(8,128)(2,1)}), bf16[16,32,3840]{2,1,0:T(8,128)(2,1)}, u32[]{:S(2)}, u32[]{:S(2)}) async-start(bf16[16,32,3840]{2,1,0:T(8,128)(2,1)} %bitcast.410), calls=%async_computation.3 | async-start | bytes 7864320 | tf_op jit(solution)/shard_map/all_to_all | solution.py:95
  239.6 5.1 %multiply_convert_fusion.1 = (bf16[480,1,16,30]{0,3,2,1:T(8,128)(2,1)S(1)}, bf16[480,1,16,30]{0,3,2,1:T(8,128)(2,1)S(1)}) fusion(s32[16,30]{1,0:T(8,128)S(1)} %multiply_add_fusion), kind=kLoop, calls=%fused_computation.67 | loop fusion | flops 3225600 | bytes 923520 | tf_op jit(solution)/shard_map/convert.36
  244.7 0.0 copy-start.1
  244.7 56.4 %all-to-all-done.3 = bf16[16,32,3840]{2,1,0:T(8,128)(2,1)} async-done(((bf16[16,32,3840]{2,1,0:T(8,128)(2,1)}), bf16[16,32,3840]{2,1,0:T(8,128)(2,1)}, u32[]{:S(2)}, u32[]{:S(2)}) %all-to-all-start.3) | async-done | bytes 3932192 | tf_op jit(solution)/shard_map/all_to_all | solution.py:95
  301.1 7.2 %reshape.1435 = bf16[16,16,2,30,128]{4,3,2,1,0:T(8,128)(2,1)} reshape(bf16[16,32,3840]{2,1,0:T(8,128)(2,1)} %all-to-all-done.3) | data formatting | bytes 7864320 | tf_op jit(solution)/shard_map/reshape | solution.py:96
  308.4 0.0 copy-done.1
  308.4 5.7 %fusion.8 = bf16[1,16,480,128]{3,2,1,0:T(8,128)(2,1)} fusion(bf16[16,16,2,30,128]{4,3,2,1,0:T(8,128)(2,1)} %reshape.1435, bf16[1,16,480,128]{3,2,1,0:T(8,128)(2,1)S(1)} %copy-done.1, bf16[480,1,16,30]{0,3,2,1:T(8,128)(2,1)S(1)} %get-tuple-element.6, bf16[480,1,16,30]{0,3,2,1:T(8,128)(2,1)S(1)} %get-tuple-element.5), kind=kOutput, calls=%fused_computation.19 | convolution fusion | flops 1892229120 | bytes 8785920 | tf_op jit(solution)/shard_map/rhpkc,wprk->hwc/dot_general | solution.py:98
  (23 shorter events, 0.7 us)
Async XLA Ops:
  12.4 68.3 %all-to-all-start = ((bf16[16,2,480,128]{3,0,1,2:T(8,128)(2,1)}), bf16[16,2,480,128]{3,0,1,2:T(8,128)(2,1)}, u32[]{:S(2)}, u32[]{:S(2)}) async-start(bf16[16,2,480,128]{3,0,1,2:T(8,128)(2,1)} %copy.10), calls=%async_computation | async-start | bytes 7864320 | tf_op jit(solution)/shard_map/all_to_all | solution.py:62
  93.8 5.1 %copy-start = (s32[8,2]{0,1:T(2,128)S(1)}, s32[8,2]{0,1:T(2,128)}, u32[]{:S(2)}) copy-start(s32[8,2]{0,1:T(2,128)} %param.5) | copy-start | bytes 196
  93.8 48.9 %all-to-all-start.1 = ((bf16[8,64,3840]{2,1,0:T(8,128)(2,1)}), bf16[8,64,3840]{2,1,0:T(8,128)(2,1)}, u32[]{:S(2)}, u32[]{:S(2)}) async-start(bf16[8,64,3840]{2,1,0:T(8,128)(2,1)} %bitcast.409), calls=%async_computation.1 | async-start | bytes 7864320 | tf_op jit(solution)/shard_map/all_to_all | solution.py:67
  232.7 68.4 %all-to-all-start.3 = ((bf16[16,32,3840]{2,1,0:T(8,128)(2,1)}), bf16[16,32,3840]{2,1,0:T(8,128)(2,1)}, u32[]{:S(2)}, u32[]{:S(2)}) async-start(bf16[16,32,3840]{2,1,0:T(8,128)(2,1)} %bitcast.410), calls=%async_computation.3 | async-start | bytes 7864320 | tf_op jit(solution)/shard_map/all_to_all | solution.py:95
  244.7 63.6 %copy-start.1 = (bf16[1,16,480,128]{3,2,1,0:T(8,128)(2,1)S(1)}, bf16[1,16,480,128]{3,2,1,0:T(8,128)(2,1)}, u32[]{:S(2)}) copy-start(bf16[1,16,480,128]{3,2,1,0:T(8,128)(2,1)} %param.3) | copy-start | bytes 5898244

commit v4 on v3

v4 whole, which is shorter than its diff:
```python
import math

import jax
import jax.numpy as jnp
from jax import lax
from jax.sharding import PartitionSpec as P


def row_table(length):
    across = jnp.arange(length, dtype=jnp.int32)
    phases = across[:, None] * across[None, :] % length
    angles = phases.astype(jnp.float32) * (2.0 * math.pi / length)
    factor = 1.0 / math.sqrt(length)
    return jnp.concatenate([jnp.cos(angles) * factor, -jnp.sin(angles) * factor], axis=1).astype(
        jnp.bfloat16
    )


def column_matrix(length, sign, row_of, col_of):
    rows = lax.broadcasted_iota(jnp.int32, (2 * length, 2 * length), 0)
    cols = lax.broadcasted_iota(jnp.int32, (2 * length, 2 * length), 1)
    k, p = row_of(rows)
    h, q = col_of(cols)
    phases = k * h % length
    angles = phases.astype(jnp.float32) * (2.0 * math.pi / length)
    factor = 1.0 / math.sqrt(length)
    cosine = jnp.cos(angles) * factor
    sine_part = sign * jnp.sin(angles) * factor
    value = jnp.where(p == q, cosine, jnp.where(p == 0, -sine_part, sine_part))
    return value.astype(jnp.bfloat16)


def interleaved(index):
    return index // 2, index % 2


def blocked(kb):
    def split(index):
        blk, rest = index // (2 * kb), index % (2 * kb)
        return blk * kb + rest % kb, rest // kb

    return split


CHUNKS = 2


def on_device(features, filters, anchors):
    frames = lax.psum(1, "gop")
    blocks = lax.psum(1, "row")
    _, hb, columns, chans = features.shape
    height = filters.shape[1]
    wb = columns // blocks
    kb = height // frames
    part = wb // CHUNKS
    lanes = part * chans
    me_gop = lax.axis_index("gop")

    table = row_table(columns).reshape(columns, 2, blocks, wb)
    forward_cols = column_matrix(height, -1.0, blocked(kb), interleaved)
    inverse_cols = column_matrix(height, 1.0, interleaved, blocked(kb))

    x = features[0]
    gains = lax.dynamic_slice_in_dim(filters, me_gop * kb, kb, axis=1)
    gains = gains.transpose(0, 2, 1, 3, 4)
    total = x.astype(jnp.float32)
    for chunk in range(CHUNKS):
        cols = slice(chunk * part, (chunk + 1) * part)
        piece = table[:, :, :, cols]
        rowwise = jnp.einsum("hwc,wprk->rhpkc", x, piece, preferred_element_type=jnp.float32)
        rowwise = rowwise.astype(jnp.bfloat16)
        slab = lax.all_to_all(rowwise, "row", 0, 0, tiled=True)
        spectra = jnp.dot(
            forward_cols, slab.reshape(2 * height, lanes), preferred_element_type=jnp.float32
        ).astype(jnp.bfloat16)
        spectra = spectra.reshape(frames, 2 * kb, lanes)
        every = lax.all_to_all(spectra, "gop", 0, 0, tiled=True)
        every = every.reshape(frames, 2, kb, lanes)
        gain = gains[:, :, :, cols].reshape(3, 2, kb, lanes).astype(jnp.float32)
        outs = []
        for frame in range(frames):
            sources = (
                every[frame],
                lax.dynamic_index_in_dim(every, anchors[frame, 0], 0, keepdims=False),
                lax.dynamic_index_in_dim(every, anchors[frame, 1], 0, keepdims=False),
            )
            real_part = jnp.zeros((kb, lanes), jnp.float32)
            imag_part = jnp.zeros((kb, lanes), jnp.float32)
            for which_one in range(3):
                source_real = sources[which_one][0].astype(jnp.float32)
                source_imag = sources[which_one][1].astype(jnp.float32)
                gain_real = gain[which_one, 0]
                gain_imag = gain[which_one, 1]
                real_part = real_part + gain_real * source_real - gain_imag * source_imag
                imag_part = imag_part + gain_real * source_imag + gain_imag * source_real
            outs.append(jnp.stack([real_part, imag_part]))
        mixed = jnp.stack(outs).astype(jnp.bfloat16).reshape(frames, 2 * kb, lanes)
        mine = lax.all_to_all(mixed, "gop", 0, 0, tiled=True)
        back = jnp.dot(
            inverse_cols, mine.reshape(2 * height, lanes), preferred_element_type=jnp.float32
        ).astype(jnp.bfloat16)
        back = back.reshape(blocks, 2 * hb, lanes)
        rows_back = lax.all_to_all(back, "row", 0, 0, tiled=True)
        rows_back = rows_back.reshape(blocks, hb, 2, part, chans)
        total = total + jnp.einsum(
            "rhpkc,wprk->hwc", rows_back, piece, preferred_element_type=jnp.float32
        )
    return total.astype(jnp.bfloat16)[None]


def solution(mesh):
    in_specs = (P("gop", "row", None, None), P(None, None, None, "row", None), P())
    out_specs = P("gop", "row", None, None)
    return jax.shard_map(
        on_device, mesh=mesh, in_specs=in_specs, out_specs=out_specs, check_vma=False
    )
```

time: 316 us -> 313 us (level)
  the two profiles are of different devices: /device:TPU:92 before, /device:TPU:0 now
where the time goes in v4:
time: 313 us; the launch traced here: 311 us
  waiting for transfers between devices  129 us (41%)
  matrix products  49.8 us (16%)
  starting transfers between devices  37.5 us (12%)
  other arithmetic  32.4 us (10%)
  local copies, waits for them, and re-layouts  32.3 us (10%)
  between operations  30.5 us (10%)
    all_to_all x2, waiting for transfers between devices, on_device(): slab = lax.all_to_all(rowwise, 'row', 0, 0, tiled=True)  41.2 us
    all_to_all x2, waiting for transfers between devices, on_device(): rows_back = lax.all_to_all(back, 'row', 0, 0, tiled=True)  37.1 us
    all_to_all x2, waiting for transfers between devices, on_device(): mine = lax.all_to_all(mixed, 'gop', 0, 0, tiled=True)  35.1 us
    another operation x33, other arithmetic  31.5 us
    dot_general x2, matrix products, on_device(): jnp.dot(inverse_cols, mine.reshape(2 * height, lanes), preferred_element_...  17.6 us
    unnamed x37, local copies, waits for them, and re-layouts  15.4 us
    all_to_all x2, waiting for transfers between devices, on_device(): every = lax.all_to_all(spectra, 'gop', 0, 0, tiled=True)  15.4 us
    dot_general x2, matrix products, on_device(): jnp.dot(forward_cols, slab.reshape(2 * height, lanes), preferred_element_...  14.6 us
  transfers between devices with their start and end apart: 8, of which 7 were waited for; matrix products, arithmetic and copies ran while one was open for 20% of the time, Pallas kernels for 0%

profile of v4, /device:TPU:0, one launch (start us, length us, event | category | flops | bytes accessed | tf_op | source)
XLA Modules:
  0.0 311.1 jit_solution(8699144652433763653)
XLA Ops:
  0.0 4.6 %multiply_convert_fusion.1 = (bf16[480,1,16,30]{0,2,3,1:T(8,128)(2,1)S(1)}, bf16[480,1,16,30]{0,2,3,1:T(8,128)(2,1)S(1)}) fusion(s32[16,30]{0,1:T(8,128)S(1)} %multiply_add_fusion), kind=kLoop, calls=%fused_computation.81 | loop fusion | flops 3225600 | bytes 923520 | tf_op jit(solution)/shard_map/convert.66
  4.7 3.1 convert_bitcast_fusion
  7.8 1.8 copy.28
  9.5 7.1 %all-to-all-start.4 = ((bf16[16,16,2,15,128]{4,1,3,2,0:T(8,128)(2,1)}), bf16[16,16,2,15,128]{4,1,3,2,0:T(8,128)(2,1)S(1)}, u32[]{:S(2)}, u32[]{:S(2)}) async-start(bf16[16,16,2,15,128]{4,1,3,2,0:T(8,128)(2,1)} %copy.28), calls=%async_computation.4 | async-start | bytes 3932160 | tf_op jit(solution)/shard_map/all_to_all | solution.py:72
  16.7 2.7 convert_bitcast_fusion.1
  19.5 1.8 copy.24
  21.3 24.2 %all-to-all-done.4 = bf16[16,16,2,15,128]{4,1,3,2,0:T(8,128)(2,1)S(1)} async-done(((bf16[16,16,2,15,128]{4,1,3,2,0:T(8,128)(2,1)}), bf16[16,16,2,15,128]{4,1,3,2,0:T(8,128)(2,1)S(1)}, u32[]{:S(2)}, u32[]{:S(2)}) %all-to-all-start.4) | async-done | bytes 1966112 | tf_op jit(solution)/shard_map/all_to_all | solution.py:72
  45.5 1.3 copy-done.4
  46.7 3.7 %all-to-all-start = ((bf16[16,16,2,15,128]{4,1,3,2,0:T(8,128)(2,1)}), bf16[16,16,2,15,128]{4,1,3,2,0:T(8,128)(2,1)S(1)}, u32[]{:S(2)}, u32[]{:S(2)}) async-start(bf16[16,16,2,15,128]{4,1,3,2,0:T(8,128)(2,1)} %copy.24), calls=%async_computation | async-start | bytes 3932160 | tf_op jit(solution)/shard_map/all_to_all | solution.py:72
  50.5 2.1 copy.29
  52.6 7.3 %convolution_convert_fusion.1 = bf16[512,1920]{1,0:T(8,128)(2,1)} fusion(bf16[64,8,15,128]{3,2,1,0:T(8,128)(2,1)S(1)} %bitcast.854, s32[512]{0:T(512)S(1)} %get-tuple-element.29, s32[512]{0:T(512)S(1)} %get-tuple-element.36, s32[512]{0:T(512)S(1)} %get-tuple-element.31, s32[512]{0:T(512)S(1)} %get-tuple-element.35, s32[512]{0:T(512)S(1)} %get-tuple-element.30, ...), kind=kOutput, calls=%fused_computation.4 | convolution fusion | flops 1019936768 | bytes 3950592 | tf_op jit(solution)/shard_map/dot_general | solution.py:73
  59.9 17.0 %all-to-all-done = bf16[16,16,2,15,128]{4,1,3,2,0:T(8,128)(2,1)S(1)} async-done(((bf16[16,16,2,15,128]{4,1,3,2,0:T(8,128)(2,1)}), bf16[16,16,2,15,128]{4,1,3,2,0:T(8,128)(2,1)S(1)}, u32[]{:S(2)}, u32[]{:S(2)}) %all-to-all-start) | async-done | bytes 1966112 | tf_op jit(solution)/shard_map/all_to_all | solution.py:72
  76.9 1.3 copy-done.2
  78.1 5.3 %all-to-all-start.5 = ((bf16[8,64,1920]{2,1,0:T(8,128)(2,1)}), bf16[8,64,1920]{2,1,0:T(8,128)(2,1)S(1)}, u32[]{:S(2)}, u32[]{:S(2)}) async-start(bf16[8,64,1920]{2,1,0:T(8,128)(2,1)} %bitcast.857), calls=%async_computation.5 | async-start | bytes 3932160 | tf_op jit(solution)/shard_map/all_to_all | solution.py:77
  83.5 2.5 constant_dynamic-slice_fusion
  86.6 7.3 %convolution_convert_fusion.3 = bf16[512,1920]{1,0:T(8,128)(2,1)} fusion(bf16[64,8,15,128]{3,2,1,0:T(8,128)(2,1)S(1)} %bitcast.855, s32[512]{0:T(512)S(1)} %get-tuple-element.29, s32[512]{0:T(512)S(1)} %get-tuple-element.36, s32[512]{0:T(512)S(1)} %get-tuple-element.31, s32[512]{0:T(512)S(1)} %get-tuple-element.35, s32[512]{0:T(512)S(1)} %get-tuple-element.30, ...), kind=kOutput, calls=%fused_computation.6 | convolution fusion | flops 1019936768 | bytes 3950592 | tf_op jit(solution)/shard_map/dot_general | solution.py:73
  93.9 15.4 %all-to-all-done.5 = bf16[8,64,1920]{2,1,0:T(8,128)(2,1)S(1)} async-done(((bf16[8,64,1920]{2,1,0:T(8,128)(2,1)}), bf16[8,64,1920]{2,1,0:T(8,128)(2,1)S(1)}, u32[]{:S(2)}, u32[]{:S(2)}) %all-to-all-start.5) | async-done | bytes 1966112 | tf_op jit(solution)/shard_map/all_to_all | solution.py:77
  109.2 1.3 copy-done
  110.5 4.3 %all-to-all-start.1 = ((bf16[8,64,1920]{2,1,0:T(8,128)(2,1)}), bf16[8,64,1920]{2,1,0:T(8,128)(2,1)}, u32[]{:S(2)}, u32[]{:S(2)}) async-start(bf16[8,64,1920]{2,1,0:T(8,128)(2,1)} %bitcast.856), calls=%async_computation.1 | async-start | bytes 3932160 | tf_op jit(solution)/shard_map/all_to_all | solution.py:77
  146.5 1.4 fusion.216
  147.9 1.4 fusion.222
  149.3 0.7 bitcast_dynamic-update-slice_fusion.7
  150.0 1.3 fusion.56
  151.4 1.4 fusion.62
  152.8 0.7 bitcast_dynamic-update-slice_fusion.15
  153.5 1.3 fusion.196
  154.8 1.4 fusion.202
  156.2 1.4 fusion.176
  157.6 1.4 fusion.182
  159.0 1.4 fusion.156
  160.3 1.4 fusion.162
  161.7 1.4 fusion.136
  163.1 1.4 fusion.142
  164.5 1.4 fusion.116
  165.9 1.4 fusion.122
  167.3 1.4 fusion.96
  168.6 1.4 fusion.102
  170.0 1.4 fusion.76
  171.4 1.4 fusion.82
  172.8 0.7 bitcast_dynamic-update-slice_fusion.14
  173.5 0.7 bitcast_dynamic-update-slice_fusion.13
  176.3 0.7 bitcast_dynamic-update-slice_fusion.9
  177.0 0.7 bitcast_dynamic-update-slice_fusion.8
  177.7 4.8 %all-to-all-start.2 = ((bf16[8,64,1920]{2,1,0:T(8,128)(2,1)}), bf16[8,64,1920]{2,1,0:T(8,128)(2,1)}, u32[]{:S(2)}, u32[]{:S(2)}) async-start(bf16[8,64,1920]{2,1,0:T(8,128)(2,1)} %bitcast_dynamic-update-slice_fusion.8), calls=%async_computation.2 | async-start | bytes 3932160 | tf_op jit(solution)/shard_map/all_to_all | solution.py:98
  185.3 0.7 bitcast_dynamic-update-slice_fusion.6
  186.0 0.7 bitcast_dynamic-update-slice_fusion.5
  186.7 0.7 bitcast_dynamic-update-slice_fusion.4
  187.4 0.7 bitcast_dynamic-update-slice_fusion.3
  188.2 0.7 bitcast_dynamic-update-slice_fusion.2
  188.9 0.7 bitcast_dynamic-update-slice_fusion.1
  190.3 18.1 %all-to-all-done.2 = bf16[8,64,1920]{2,1,0:T(8,128)(2,1)} async-done(((bf16[8,64,1920]{2,1,0:T(8,128)(2,1)}), bf16[8,64,1920]{2,1,0:T(8,128)(2,1)}, u32[]{:S(2)}, u32[]{:S(2)}) %all-to-all-start.2) | async-done | bytes 1966112 | tf_op jit(solution)/shard_map/all_to_all | solution.py:98
  208.4 3.6 %all-to-all-start.6 = ((bf16[8,64,1920]{2,1,0:T(8,128)(2,1)}), bf16[8,64,1920]{2,1,0:T(8,128)(2,1)S(1)}, u32[]{:S(2)}, u32[]{:S(2)}) async-start(bf16[8,64,1920]{2,1,0:T(8,128)(2,1)} %bitcast_dynamic-update-slice_fusion), calls=%async_computation.6 | async-start | bytes 3932160 | tf_op jit(solution)/shard_map/all_to_all | solution.py:98
  212.0 8.7 %convolution_convert_fusion.2 = bf16[512,1920]{1,0:T(8,128)(2,1)} fusion(bf16[512,1920]{1,0:T(8,128)(2,1)} %bitcast.100, s32[512]{0:T(512)S(1)} %get-tuple-element.31, s32[512]{0:T(512)S(1)} %get-tuple-element.35, s32[512]{0:T(512)S(1)} %get-tuple-element.29, s32[512]{0:T(512)S(1)} %get-tuple-element.36, s32[512]{0:T(512)S(1)} %get-tuple-element.32, ...), kind=kOutput, calls=%fused_computation.5 | convolution fusion | flops 1019936768 | bytes 3950592 | tf_op jit(solution)/shard_map/dot_general | solution.py:99
  220.8 16.9 %all-to-all-done.6 = bf16[8,64,1920]{2,1,0:T(8,128)(2,1)S(1)} async-done(((bf16[8,64,1920]{2,1,0:T(8,128)(2,1)}), bf16[8,64,1920]{2,1,0:T(8,128)(2,1)S(1)}, u32[]{:S(2)}, u32[]{:S(2)}) %all-to-all-start.6) | async-done | bytes 1966112 | tf_op jit(solution)/shard_map/all_to_all | solution.py:98
  237.7 1.3 copy-done.5
  239.0 3.8 %all-to-all-start.3 = ((bf16[16,32,1920]{2,1,0:T(8,128)(2,1)}), bf16[16,32,1920]{2,1,0:T(8,128)(2,1)S(1)}, u32[]{:S(2)}, u32[]{:S(2)}) async-start(bf16[16,32,1920]{2,1,0:T(8,128)(2,1)} %bitcast.860), calls=%async_computation.3 | async-start | bytes 3932160 | tf_op jit(solution)/shard_map/all_to_all | solution.py:103
  242.8 8.8 %convolution_convert_fusion = bf16[512,1920]{1,0:T(8,128)(2,1)} fusion(bf16[512,1920]{1,0:T(8,128)(2,1)} %bitcast.858, s32[512]{0:T(512)S(1)} %get-tuple-element.31, s32[512]{0:T(512)S(1)} %get-tuple-element.35, s32[512]{0:T(512)S(1)} %get-tuple-element.29, s32[512]{0:T(512)S(1)} %get-tuple-element.36, s32[512]{0:T(512)S(1)} %get-tuple-element.32, ...), kind=kOutput, calls=%fused_computation.3 | convolution fusion | flops 1019936768 | bytes 3950592 | tf_op jit(solution)/shard_map/dot_general | solution.py:99
  251.7 19.6 %all-to-all-done.3 = bf16[16,32,1920]{2,1,0:T(8,128)(2,1)S(1)} async-done(((bf16[16,32,1920]{2,1,0:T(8,128)(2,1)}), bf16[16,32,1920]{2,1,0:T(8,128)(2,1)S(1)}, u32[]{:S(2)}, u32[]{:S(2)}) %all-to-all-start.3) | async-done | bytes 1966112 | tf_op jit(solution)/shard_map/all_to_all | solution.py:103
  271.2 4.7 %all-to-all-start.7 = ((bf16[16,32,1920]{2,1,0:T(8,128)(2,1)}), bf16[16,32,1920]{2,1,0:T(8,128)(2,1)}, u32[]{:S(2)}, u32[]{:S(2)}) async-start(bf16[16,32,1920]{2,1,0:T(8,128)(2,1)} %bitcast.859), calls=%async_computation.7 | async-start | bytes 3932160 | tf_op jit(solution)/shard_map/all_to_all | solution.py:103
  275.9 2.6 reshape.2804
  278.5 5.4 %fusion.10 = f32[480,16,128,1,1]{2,0,3,1,4:T(8,128)} fusion(bf16[16,16,2,15,128]{4,3,2,1,0:T(8,128)(2,1)} %reshape.2804, bf16[480,1,16,30]{0,2,3,1:T(8,128)(2,1)S(1)} %copy-done.7, bf16[480,1,16,30]{0,2,3,1:T(8,128)(2,1)S(1)} %copy-done.9), kind=kOutput, calls=%fused_computation.24 | convolution fusion | flops 944640000 | bytes 6819840 | tf_op jit(solution)/shard_map/rhpkc,wprk->hwc/dot_general | solution.py:105
  283.9 17.5 %all-to-all-done.7 = bf16[16,32,1920]{2,1,0:T(8,128)(2,1)} async-done(((bf16[16,32,1920]{2,1,0:T(8,128)(2,1)}), bf16[16,32,1920]{2,1,0:T(8,128)(2,1)}, u32[]{:S(2)}, u32[]{:S(2)}) %all-to-all-start.7) | async-done | bytes 1966112 | tf_op jit(solution)/shard_map/all_to_all | solution.py:103
  301.4 3.3 %reshape.2810 = bf16[16,16,2,15,128]{4,3,2,1,0:T(8,128)(2,1)S(1)} reshape(bf16[16,32,1920]{2,1,0:T(8,128)(2,1)} %all-to-all-done.7) | data formatting | bytes 3932160 | tf_op jit(solution)/shard_map/reshape | solution.py:104
  304.7 6.5 %fusion.16 = bf16[1,16,480,128]{3,2,1,0:T(8,128)(2,1)} fusion(bf16[16,16,2,15,128]{4,3,2,1,0:T(8,128)(2,1)S(1)} %reshape.2810, f32[480,16,128,1,1]{2,0,3,1,4:T(8,128)} %fusion.10, bf16[1,16,480,128]{3,2,1,0:T(8,128)(2,1)} %param.3, bf16[480,1,16,30]{0,2,3,1:T(8,128)(2,1)S(1)} %copy-done.9, bf16[480,1,16,30]{0,2,3,1:T(8,128)(2,1)S(1)} %copy-done.7), kind=kOutput, calls=%fused_computation.28 | convolution fusion | flops 948572160 | bytes 10752000 | tf_op jit(solution)/shard_map/rhpkc,wprk->hwc/dot_general | solution.py:105
  (66 shorter events, 7.9 us)
Async XLA Ops:
  4.6 12.0 %copy-start.6 = (bf16[480,1,16,30]{0,2,3,1:T(8,128)(2,1)}, bf16[480,1,16,30]{0,2,3,1:T(8,128)(2,1)S(1)}, u32[]{:S(2)}) copy-start(bf16[480,1,16,30]{0,2,3,1:T(8,128)(2,1)S(1)} %get-tuple-element.7) | copy-start | bytes 1382404
  4.7 12.0 %copy-start.8 = (bf16[480,1,16,30]{0,2,3,1:T(8,128)(2,1)}, bf16[480,1,16,30]{0,2,3,1:T(8,128)(2,1)S(1)}, u32[]{:S(2)}) copy-start(bf16[480,1,16,30]{0,2,3,1:T(8,128)(2,1)S(1)} %get-tuple-element.8) | copy-start | bytes 1382404
  9.5 35.9 %all-to-all-start.4 = ((bf16[16,16,2,15,128]{4,1,3,2,0:T(8,128)(2,1)}), bf16[16,16,2,15,128]{4,1,3,2,0:T(8,128)(2,1)S(1)}, u32[]{:S(2)}, u32[]{:S(2)}) async-start(bf16[16,16,2,15,128]{4,1,3,2,0:T(8,128)(2,1)} %copy.28), calls=%async_computation.4 | async-start | bytes 3932160 | tf_op jit(solution)/shard_map/all_to_all | solution.py:72
  45.5 1.3 copy-start.4
  46.7 30.1 %all-to-all-start = ((bf16[16,16,2,15,128]{4,1,3,2,0:T(8,128)(2,1)}), bf16[16,16,2,15,128]{4,1,3,2,0:T(8,128)(2,1)S(1)}, u32[]{:S(2)}, u32[]{:S(2)}) async-start(bf16[16,16,2,15,128]{4,1,3,2,0:T(8,128)(2,1)} %copy.24), calls=%async_computation | async-start | bytes 3932160 | tf_op jit(solution)/shard_map/all_to_all | solution.py:72
  76.9 1.3 copy-start.2
  78.1 31.1 %all-to-all-start.5 = ((bf16[8,64,1920]{2,1,0:T(8,128)(2,1)}), bf16[8,64,1920]{2,1,0:T(8,128)(2,1)S(1)}, u32[]{:S(2)}, u32[]{:S(2)}) async-start(bf16[8,64,1920]{2,1,0:T(8,128)(2,1)} %bitcast.857), calls=%async_computation.5 | async-start | bytes 3932160 | tf_op jit(solution)/shard_map/all_to_all | solution.py:77
  83.5 2.5 copy-start.3
  109.2 1.3 copy-start
  109.2 5.6 %copy-start.10 = (s32[8,2]{0,1:T(2,128)S(1)}, s32[8,2]{0,1:T(2,128)}, u32[]{:S(2)}) copy-start(s32[8,2]{0,1:T(2,128)} %param.5) | copy-start | bytes 196
  110.5 39.5 %all-to-all-start.1 = ((bf16[8,64,1920]{2,1,0:T(8,128)(2,1)}), bf16[8,64,1920]{2,1,0:T(8,128)(2,1)}, u32[]{:S(2)}, u32[]{:S(2)}) async-start(bf16[8,64,1920]{2,1,0:T(8,128)(2,1)} %bitcast.856), calls=%async_computation.1 | async-start | bytes 3932160 | tf_op jit(solution)/shard_map/all_to_all | solution.py:77
  177.7 4.8 %copy-start.1 = (bf16[8,64,1920]{2,1,0:T(8,128)(2,1)S(1)}, bf16[8,64,1920]{2,1,0:T(8,128)(2,1)}, u32[]{:S(2)}) copy-start(bf16[8,64,1920]{2,1,0:T(8,128)(2,1)} %copy-done) | copy-start | bytes 5898244
  177.7 30.7 %all-to-all-start.2 = ((bf16[8,64,1920]{2,1,0:T(8,128)(2,1)}), bf16[8,64,1920]{2,1,0:T(8,128)(2,1)}, u32[]{:S(2)}, u32[]{:S(2)}) async-start(bf16[8,64,1920]{2,1,0:T(8,128)(2,1)} %bitcast_dynamic-update-slice_fusion.8), calls=%async_computation.2 | async-start | bytes 3932160 | tf_op jit(solution)/shard_map/all_to_all | solution.py:98
  208.4 29.3 %all-to-all-start.6 = ((bf16[8,64,1920]{2,1,0:T(8,128)(2,1)}), bf16[8,64,1920]{2,1,0:T(8,128)(2,1)S(1)}, u32[]{:S(2)}, u32[]{:S(2)}) async-start(bf16[8,64,1920]{2,1,0:T(8,128)(2,1)} %bitcast_dynamic-update-slice_fusion), calls=%async_computation.6 | async-start | bytes 3932160 | tf_op jit(solution)/shard_map/all_to_all | solution.py:98
  237.7 1.3 copy-start.5
  239.0 32.2 %all-to-all-start.3 = ((bf16[16,32,1920]{2,1,0:T(8,128)(2,1)}), bf16[16,32,1920]{2,1,0:T(8,128)(2,1)S(1)}, u32[]{:S(2)}, u32[]{:S(2)}) async-start(bf16[16,32,1920]{2,1,0:T(8,128)(2,1)} %bitcast.860), calls=%async_computation.3 | async-start | bytes 3932160 | tf_op jit(solution)/shard_map/all_to_all | solution.py:103
  271.2 30.2 %all-to-all-start.7 = ((bf16[16,32,1920]{2,1,0:T(8,128)(2,1)}), bf16[16,32,1920]{2,1,0:T(8,128)(2,1)}, u32[]{:S(2)}, u32[]{:S(2)}) async-start(bf16[16,32,1920]{2,1,0:T(8,128)(2,1)} %bitcast.859), calls=%async_computation.7 | async-start | bytes 3932160 | tf_op jit(solution)/shard_map/all_to_all | solution.py:103
  275.9 2.6 copy-start.7
  275.9 2.6 copy-start.9
